TPU v7x, 512 devices: a whole 4x4x16 slice. The times are simulated.
512 devices in a mesh: node: 32 (over z, core), feat: 16 (over x, y).
Axes of the slice: x: 4, y: 4, z: 16, core: 2. Of those that a mesh axis runs over, the one named last changes fastest.
Arguments:
- covariates: bfloat16 [256, 131072], P('feat', 'node'), may hold values from 0 to 0.9921875
- pseudo: bfloat16 [16, 131072], P(None, 'node'), may hold values from -6 to 6
- honest: int32 [131072], P('node'), may hold values 0 or 1
- destination: int32 [131072, 1], P('node'), may hold values from 0 to 63; in each aligned block of 4096 rows (0 to 4095, 4096 to 8191, ...) at most 128 rows name the same one
- node_slot: int32 [64], replicated, may hold values from 0 to 63, each once
Outputs:
- histogram: float32 [64, 256, 17, 256], P('node', 'feat')
- best_gain: float32 [64], P('node')
Inputs may be any that keep to these rules, and one draw needn't show every extreme that they name: `destination`: in the rows of one device no child node is named by more than 128 rows. Each slot appears once; child node n belongs to the owner node_slot[n] // 2 along node.
All inputs are finite; a program needn't handle non-finite values. No bound on the sum of `honest` on one device may be relied on, other than what follows from the above.
Results may differ from a plain program's by a relative error of at most 0.0003.
Values may be sent and summed in bfloat16 or wider, within the bound.
No kernel may reach another device: no remote copies, remote signals or barrier semaphores. Data moves between devices by JAX's collectives and lax.ppermute only.
A program may use at most 64 MiB of HBM per device.

v0:
```python
import jax
import jax.numpy as jnp
from jax import lax
from jax.sharding import PartitionSpec as P

B = 256


def feature_histograms(bin_table, statistics):
    levels = lax.broadcasted_iota(jnp.int32, (1, 1, B), 2)

    def one_feature(bin_row):
        indicator = (bin_row[:, :, None] == levels).astype(jnp.bfloat16)
        return jnp.einsum("skr,krb->ksb", statistics, indicator, preferred_element_type=jnp.float32)

    stacked = lax.map(one_feature, bin_table)
    return jnp.transpose(stacked, (1, 0, 2, 3))


def on_device(covariates, pseudo, honest, destination, node_slot):
    feat_count, row_count = covariates.shape
    node_devices = lax.axis_size("node")
    node_total = node_slot.shape[0]
    node_local = node_total // node_devices
    capacity = 2 * row_count // node_total
    weight = (1 - honest).astype(jnp.float32)
    columns = lax.broadcasted_iota(jnp.int32, (1, node_total), 1)
    named = (destination == columns).astype(jnp.int32)
    target = jnp.sum(named * node_slot[None, :], axis=1)
    owned = (target[:, None] == columns).astype(jnp.int32)
    rank = jnp.sum((jnp.cumsum(owned, axis=0) - 1) * owned, axis=1)
    position = target * capacity + rank
    weighted = weight[None, :] * pseudo.astype(jnp.float32)
    weight_row = weight[None, :].astype(jnp.bfloat16)
    payload = jnp.concatenate([covariates, weight_row, weighted.astype(jnp.bfloat16)], axis=0)
    payload_width = payload.shape[0]
    outgoing = (
        jnp.zeros((payload_width, node_total * capacity), jnp.bfloat16).at[:, position].set(payload)
    )
    outgoing = outgoing.reshape(payload_width, node_devices, node_local, capacity)
    arrived = lax.all_to_all(outgoing, "node", split_axis=1, concat_axis=3, tiled=True)[:, 0]
    bin_table = jnp.floor(arrived[:feat_count].astype(jnp.float32) * B).astype(jnp.int32)
    statistics = arrived[feat_count:]
    histogram = feature_histograms(bin_table, statistics)
    left = jnp.cumsum(histogram, axis=3)
    total = left[:, :, :, -1:]
    right = total - left
    left_part = jnp.sum(left[:, :, 1:] * left[:, :, 1:], axis=2) / (left[:, :, 0] + 1.0)
    right_part = jnp.sum(right[:, :, 1:] * right[:, :, 1:], axis=2) / (right[:, :, 0] + 1.0)
    total_part = jnp.sum(total[:, :, 1:] * total[:, :, 1:], axis=2) / (total[:, :, 0] + 1.0)
    gain = left_part + right_part - total_part
    best_local = jnp.max(gain, axis=(1, 2))
    best_gain = lax.pmax(best_local, "feat")
    return (histogram, best_gain)


def solution(mesh):
    placed = (P("feat", "node"), P(None, "node"), P("node"), P("node", None), P())
    return jax.shard_map(
        on_device,
        mesh=mesh,
        in_specs=placed,
        out_specs=(P("node", "feat", None, None), P("node")),
        check_vma=False,
    )
```

profile of v0, /device:TPU:32, one launch (start us, length us, event | category | flops | bytes accessed | tf_op | source)
XLA Modules:
  0.0 179.9 jit_solution(6123382762553498424)
XLA Ops:
  0.6 1.0 select_reduce_fusion
  1.7 18.4 %reduce-window.14 = s32[64,32,128]{2,1,0:T(8,128)S(1)} reduce-window(s32[64,32,128]{2,1,0:T(8,128)S(1)} %fusion.9, s32[]{:T(128)} %constant.16.clone.1), window={size=1x1x128 pad=0_0x0_0x127_0}, to_apply=%region_1.0 | reduce-window | flops 33292288 | bytes 2097156 | tf_op jit(solution)/shard_map/reduce-window
  20.2 0.3 slice.62
  20.5 0.4 copy.87
  21.0 0.2 reduce-window.15
  21.2 0.3 add_add_fusion
  21.5 0.8 fusion.6
  22.5 0.5 copy.72
  23.0 11.6 %scatter_custom_fusion = bf16[33,8192]{0,1:T(8,128)(2,1)S(1)} fusion(s32[4096]{0:T(1024)S(1)} %bitcast.103, bf16[4096,33]{1,0:T(8,128)(2,1)S(1)} %copy.72, bf16[]{:T(256)} %constant.18.clone.1), kind=kCustom, calls=%fused_computation.15 | custom fusion | bytes 540674 | tf_op jit(solution)/shard_map/scatter | solution.py:38
  34.6 2.6 %copy.73 = bf16[33,32,2,128]{3,2,0,1:T(2,128)(2,1)} copy(bf16[33,32,2,128]{0,3,2,1:T(8,128)(2,1)S(1)} %bitcast.91) | data formatting | bytes 1081344 | tf_op jit(solution)/shard_map/reshape | solution.py:40
  37.2 15.4 %all-to-all-start = ((bf16[33,32,2,128]{3,2,0,1:T(2,128)(2,1)}), bf16[33,32,2,128]{3,2,0,1:T(2,128)(2,1)S(1)}, u32[]{:S(2)}, u32[]{:S(2)}) async-start(bf16[33,32,2,128]{3,2,0,1:T(2,128)(2,1)} %copy.73), calls=%async_computation | async-start | bytes 1081344 | tf_op jit(solution)/shard_map/all_to_all | solution.py:41
  52.6 32.9 %all-to-all-done = bf16[33,32,2,128]{3,2,0,1:T(2,128)(2,1)S(1)} async-done(((bf16[33,32,2,128]{3,2,0,1:T(2,128)(2,1)}), bf16[33,32,2,128]{3,2,0,1:T(2,128)(2,1)S(1)}, u32[]{:S(2)}, u32[]{:S(2)}) %all-to-all-start) | async-done | bytes 540704 | tf_op jit(solution)/shard_map/all_to_all | solution.py:41
  85.7 0.3 reshape.104
  86.1 0.2 copy.77
  86.3 30.2 %while.11 = (s32[]{:T(128)}, f32[16,2,17,256]{3,0,2,1:T(8,128)S(1)}, s32[16,2,4096]{2,1,0:T(2,128)S(1)}, bf16[17,2,4096]{2,0,1:T(8,128)(2,1)S(1)}, s32[]{:T(128)}, /*index=5*/s32[]{:T(128)}) while((s32[]{:T(128)}, f32[16,2,17,256]{3,0,2,1:T(8,128)S(1)}, s32[16,2,4096]{2,1,0:T(2,128)S(1)}, bf16[17,2,4096]{2,0,1:T(8,128)(2,1)S(1)}, ...), condition=%wide.region_6.7_spmd.clone, body=%wide.region_5.6_spmd.clone.sunk | while | flops 73400320 | bytes 550989 | solution.py:16
  86.3 1.6 fusion.29
  88.2 1.6 fusion.29
  90.1 1.6 fusion.29
  91.9 1.6 fusion.29
  93.8 1.6 fusion.29
  95.7 1.6 fusion.29
  97.4 0.2 dynamic_update_slice.6
  97.6 1.6 fusion.29
  99.3 0.2 dynamic_update_slice.6
  99.5 1.6 fusion.29
  101.2 0.2 dynamic_update_slice.6
  101.4 1.6 fusion.29
  103.3 1.6 fusion.29
  105.2 1.6 fusion.29
  107.0 1.6 fusion.29
  108.9 1.6 fusion.29
  110.8 1.6 fusion.29
  112.7 1.6 fusion.29
  114.6 1.6 fusion.29
  116.5 0.3 reshape.94
  116.8 0.3 copy.79
  117.1 18.4 %reduce-window.16 = f32[2,16,17,2,128]{4,2,3,1,0:T(8,128)S(1)} reduce-window(f32[2,16,17,2,128]{4,2,3,1,0:T(8,128)S(1)} %copy.79, f32[]{:T(128)} %constant.9.clone.1), window={size=1x1x1x1x128 pad=0_0x0_0x0_0x0_0x127_0}, to_apply=%region_7.8 | reduce-window | flops 17686528 | bytes 1114116 | tf_op jit(solution)/shard_map/reduce-window.2
  135.5 0.3 slice.66
  135.7 0.5 copy.80
  136.4 0.3 broadcast_add_fusion
  136.7 0.3 copy.82
  137.0 0.4 reduce_window_sum.30
  137.4 0.2 fusion.12
  137.6 0.2 fusion.23
  137.9 0.3 copy.89
  138.3 0.2 broadcast_subtract_fusion
  138.6 0.2 fusion.22
  138.7 41.1 %pmax.7 = f32[2]{0:T(128)} all-reduce(f32[2]{0:T(128)S(1)} %fusion.22), channel_id=1, replica_groups=mesh['node'=32,'feat'=16] {'feat'}, use_global_device_ids=true, to_apply=%region_13.14 | all-reduce | flops 2 | bytes 16 | tf_op jit(solution)/shard_map/pmax | solution.py:53
  (71 shorter events, 3.8 us)
Async XLA Ops:
  20.5 1.9 %copy-start.3 = (s32[4096]{0:T(1024)S(1)}, s32[4096]{0:T(1024)}, u32[]{:S(2)}) copy-start(s32[4096]{0:T(1024)} %param.9) | copy-start | bytes 49156
  20.5 1.9 %copy-start.2 = (bf16[16,4096]{1,0:T(8,128)(2,1)S(1)}, bf16[16,4096]{1,0:T(8,128)(2,1)}, u32[]{:S(2)}) copy-start(bf16[16,4096]{1,0:T(8,128)(2,1)} %param.8) | copy-start | bytes 393220
  21.0 1.5 copy-start.1
  37.2 48.2 %all-to-all-start = ((bf16[33,32,2,128]{3,2,0,1:T(2,128)(2,1)}), bf16[33,32,2,128]{3,2,0,1:T(2,128)(2,1)S(1)}, u32[]{:S(2)}, u32[]{:S(2)}) async-start(bf16[33,32,2,128]{3,2,0,1:T(2,128)(2,1)} %copy.73), calls=%async_computation | async-start | bytes 1081344 | tf_op jit(solution)/shard_map/all_to_all | solution.py:41
  116.5 19.3 %copy-start = (f32[16,2,17,256]{3,0,2,1:T(8,128)}, f32[16,2,17,256]{3,0,2,1:T(8,128)S(1)}, u32[]{:S(2)}) copy-start(f32[16,2,17,256]{3,0,2,1:T(8,128)S(1)} %get-tuple-element.29) | copy-start | bytes 1671172
where the time goes:
time: 180 us
  blocking collectives  41.1 us (23%)
  other arithmetic  40.7 us (23%)
  waiting for transfers between devices  32.9 us (18%)
  matrix products  26.2 us (15%)
  local copies, waits for them, and re-layouts  22 us (12%)
  starting transfers between devices  15.4 us (9%)
    pmax x1, blocking collectives, on_device(): best_gain = lax.pmax(best_local, 'feat')  41.1 us
    another operation x5, other arithmetic  37.4 us
    all_to_all x1, waiting for transfers between devices, on_device(): lax.all_to_all(outgoing, 'node', split_axis=1, concat_axis=3, tiled=True)  32.9 us
    dot_general x16, matrix products, one_feature(): jnp.einsum('skr,krb->ksb', statistics, indicator, preferred_element_type=...  26.2 us
    all_to_all x1, starting transfers between devices, on_device(): lax.all_to_all(outgoing, 'node', split_axis=1, concat_axis=3, tiled=True)  15.4 us
    scatter x1, local copies, waits for them, and re-layouts, on_device(): jnp.zeros((payload_width, node_total * capacity), jnp.bfloat16)  11.6 us
  transfers between devices with their start and end apart: 1, of which 1 were waited for; matrix products, arithmetic and copies ran while one was open for 0% of the time, Pallas kernels for 0%

commit v1 on v0

--- a/solution.py
+++ b/solution.py
@@ -4,6 +4,7 @@
 from jax.sharding import PartitionSpec as P
 
 B = 256
+BLOCK = 256
 
 
 def feature_histograms(bin_table, statistics):
@@ -17,9 +18,28 @@
     return jnp.transpose(stacked, (1, 0, 2, 3))
 
 
+def running_rank(owned):
+    rows, nodes = owned.shape
+    blocks = rows // BLOCK
+    ob = owned.reshape(blocks, BLOCK, nodes).astype(jnp.bfloat16)
+    i = lax.broadcasted_iota(jnp.int32, (BLOCK, BLOCK), 0)
+    j = lax.broadcasted_iota(jnp.int32, (BLOCK, BLOCK), 1)
+    lower = (i >= j).astype(jnp.bfloat16)
+    within = jnp.einsum("ij,bjn->bin", lower, ob, preferred_element_type=jnp.float32)
+    totals = within[:, -1, :]
+    a = lax.broadcasted_iota(jnp.int32, (blocks, blocks), 0)
+    c = lax.broadcasted_iota(jnp.int32, (blocks, blocks), 1)
+    before = (a > c).astype(jnp.float32)
+    prefix = jnp.einsum("ac,cn->an", before, totals, precision=lax.Precision.HIGHEST)
+    counts = within + prefix[:, None, :]
+    mine = jnp.sum(counts * ob.astype(jnp.float32), axis=2).reshape(rows)
+    return mine.astype(jnp.int32) - 1
+
+
 def on_device(covariates, pseudo, honest, destination, node_slot):
     feat_count, row_count = covariates.shape
     node_devices = lax.axis_size("node")
+    feat_devices = lax.axis_size("feat")
     node_total = node_slot.shape[0]
     node_local = node_total // node_devices
     capacity = 2 * row_count // node_total
@@ -28,7 +48,7 @@
     named = (destination == columns).astype(jnp.int32)
     target = jnp.sum(named * node_slot[None, :], axis=1)
     owned = (target[:, None] == columns).astype(jnp.int32)
-    rank = jnp.sum((jnp.cumsum(owned, axis=0) - 1) * owned, axis=1)
+    rank = running_rank(owned)
     position = target * capacity + rank
     weighted = weight[None, :] * pseudo.astype(jnp.float32)
     weight_row = weight[None, :].astype(jnp.bfloat16)
@@ -42,7 +62,10 @@
     bin_table = jnp.floor(arrived[:feat_count].astype(jnp.float32) * B).astype(jnp.int32)
     statistics = arrived[feat_count:]
     histogram = feature_histograms(bin_table, statistics)
-    left = jnp.cumsum(histogram, axis=3)
+    c = lax.broadcasted_iota(jnp.int32, (B, B), 0)
+    b = lax.broadcasted_iota(jnp.int32, (B, B), 1)
+    upper = (c <= b).astype(jnp.float32)
+    left = jnp.einsum("nfsc,cb->nfsb", histogram, upper, precision=lax.Precision.HIGHEST)
     total = left[:, :, :, -1:]
     right = total - left
     left_part = jnp.sum(left[:, :, 1:] * left[:, :, 1:], axis=2) / (left[:, :, 0] + 1.0)
@@ -50,7 +73,9 @@
     total_part = jnp.sum(total[:, :, 1:] * total[:, :, 1:], axis=2) / (total[:, :, 0] + 1.0)
     gain = left_part + right_part - total_part
     best_local = jnp.max(gain, axis=(1, 2))
-    best_gain = lax.pmax(best_local, "feat")
+    spread = jnp.broadcast_to(best_local[None, :], (feat_devices, node_local))
+    gathered = lax.all_to_all(spread, "feat", split_axis=0, concat_axis=0, tiled=True)
+    best_gain = jnp.max(gathered, axis=0)
     return (histogram, best_gain)
 
 

time: 180 us -> 113 us (0.63)
  the two profiles are of different devices: /device:TPU:32 before, /device:TPU:1 now
where the time goes in v1:
time: 113 us
  waiting for transfers between devices  39.5 us (35%)
  matrix products  27.3 us (24%)
  starting transfers between devices  23.5 us (21%)
  local copies, waits for them, and re-layouts  18 us (16%)
  other arithmetic  3.57 us (3%)
    all_to_all x1, waiting for transfers between devices, on_device(): lax.all_to_all(outgoing, 'node', split_axis=1, concat_axis=3, tiled=True)  34.2 us
    dot_general x16, matrix products, one_feature(): jnp.einsum('skr,krb->ksb', statistics, indicator, preferred_element_type=...  26.3 us
    all_to_all x1, starting transfers between devices, on_device(): lax.all_to_all(outgoing, 'node', split_axis=1, concat_axis=3, tiled=True)  16.7 us
    scatter x1, local copies, waits for them, and re-layouts, on_device(): jnp.zeros((payload_width, node_total * capacity), jnp.bfloat16)  11.6 us
    all_to_all x1, starting transfers between devices, on_device(): lax.all_to_all(spread, 'feat', split_axis=0, concat_axis=0, tiled=True)  6.76 us
    all_to_all x1, waiting for transfers between devices, on_device(): lax.all_to_all(spread, 'feat', split_axis=0, concat_axis=0, tiled=True)  5.27 us
    reshape x1, local copies, waits for them, and re-layouts, on_device(): outgoing.reshape(payload_width, node_devices, node_local, capacity)  2.62 us
  transfers between devices with their start and end apart: 2, of which 2 were waited for; matrix products, arithmetic and copies ran while one was open for 1% of the time, Pallas kernels for 0%

profile of v1, /device:TPU:1, one launch (start us, length us, event | category | flops | bytes accessed | tf_op | source)
XLA Modules:
  0.0 113.1 jit_solution(11421704215336448270)
XLA Ops:
  0.6 0.0 copy-start.2
  0.6 0.0 copy-start.1
  0.7 0.0 copy-start
  0.7 1.0 select_reduce_fusion
  1.7 0.3 convolution_bitcast_fusion
  2.0 0.4 slice_reduce_fusion
  2.4 0.1 fusion.24
  2.6 0.3 multiply_reduce_fusion
  3.0 0.1 maximum_bitcast_fusion
  3.1 0.5 copy.60
  3.6 11.6 %scatter_custom_fusion = bf16[33,8192]{0,1:T(8,128)(2,1)S(1)} fusion(s32[4096]{0:T(1024)S(1)} %bitcast.75, bf16[4096,33]{1,0:T(8,128)(2,1)S(1)} %copy.60, bf16[]{:T(256)} %constant.18.clone.1), kind=kCustom, calls=%fused_computation.14 | custom fusion | bytes 540674 | tf_op jit(solution)/shard_map/scatter | solution.py:58
  15.2 2.6 %copy.61 = bf16[33,32,2,128]{3,2,0,1:T(2,128)(2,1)} copy(bf16[33,32,2,128]{0,3,2,1:T(8,128)(2,1)S(1)} %bitcast.69) | data formatting | bytes 1081344 | tf_op jit(solution)/shard_map/reshape | solution.py:60
  17.8 16.7 %all-to-all-start = ((bf16[33,32,2,128]{3,2,0,1:T(2,128)(2,1)}), bf16[33,32,2,128]{3,2,0,1:T(2,128)(2,1)S(1)}, u32[]{:S(2)}, u32[]{:S(2)}) async-start(bf16[33,32,2,128]{3,2,0,1:T(2,128)(2,1)} %copy.61), calls=%async_computation | async-start | bytes 1081344 | tf_op jit(solution)/shard_map/all_to_all | solution.py:61
  34.6 34.2 %all-to-all-done = bf16[33,32,2,128]{3,2,0,1:T(2,128)(2,1)S(1)} async-done(((bf16[33,32,2,128]{3,2,0,1:T(2,128)(2,1)}), bf16[33,32,2,128]{3,2,0,1:T(2,128)(2,1)S(1)}, u32[]{:S(2)}, u32[]{:S(2)}) %all-to-all-start) | async-done | bytes 540704 | tf_op jit(solution)/shard_map/all_to_all | solution.py:61
  68.8 0.1 copy.97
  68.9 0.1 floor_convert_fusion
  69.0 0.3 reshape.104
  69.3 0.1 slice.42
  69.4 0.2 copy.65
  69.5 26.9 %while.11 = (s32[]{:T(128)}, f32[16,2,17,256]{3,2,1,0:T(8,128)S(1)}, s32[16,2,4096]{2,1,0:T(2,128)S(1)}, bf16[17,2,4096]{2,0,1:T(8,128)(2,1)S(1)}, s32[]{:T(128)}) while((s32[]{:T(128)}, f32[16,2,17,256]{3,2,1,0:T(8,128)S(1)}, s32[16,2,4096]{2,1,0:T(2,128)S(1)}, bf16[17,2,4096]{2,0,1:T(8,128)(2,1)S(1)}, s32[]{:T(128)}) %tuple.33), condition=%wide.region_4.5_spmd.clone, body=%wide.region_3.4_spmd.clone.sunk | while | flops 73400320 | bytes 540741 | solution.py:17
  69.6 1.6 %fusion.32 = f32[16,2,17,256]{3,2,1,0:T(8,128)S(1)} fusion(f32[16,2,17,256]{3,2,1,0:T(8,128)S(1)} %get-tuple-element.107, s32[]{:T(128)} %get-tuple-element.106, bf16[17,2,4096]{2,0,1:T(8,128)(2,1)S(1)} %get-tuple-element.114, s32[2,4096]{1,0:T(2,128)S(1)} %dynamic-slice_bitcast_fusion.2), kind=kOutput, calls=%fused_computation.6.clone.1 | convolution fusion | flops 73400320 | bytes 475140 | tf_op jit(solution)/shard_map/while/body/eval_jaxpr/skr,krb->ksb/dot_general | solution.py:15
  71.2 1.6 %fusion.32 = f32[16,2,17,256]{3,2,1,0:T(8,128)S(1)} fusion(f32[16,2,17,256]{3,2,1,0:T(8,128)S(1)} %get-tuple-element.107, s32[]{:T(128)} %get-tuple-element.106, bf16[17,2,4096]{2,0,1:T(8,128)(2,1)S(1)} %get-tuple-element.114, s32[2,4096]{1,0:T(2,128)S(1)} %dynamic-slice_bitcast_fusion.2), kind=kOutput, calls=%fused_computation.6.clone.1 | convolution fusion | flops 73400320 | bytes 475140 | tf_op jit(solution)/shard_map/while/body/eval_jaxpr/skr,krb->ksb/dot_general | solution.py:15
  72.9 1.6 %fusion.32 = f32[16,2,17,256]{3,2,1,0:T(8,128)S(1)} fusion(f32[16,2,17,256]{3,2,1,0:T(8,128)S(1)} %get-tuple-element.107, s32[]{:T(128)} %get-tuple-element.106, bf16[17,2,4096]{2,0,1:T(8,128)(2,1)S(1)} %get-tuple-element.114, s32[2,4096]{1,0:T(2,128)S(1)} %dynamic-slice_bitcast_fusion.2), kind=kOutput, calls=%fused_computation.6.clone.1 | convolution fusion | flops 73400320 | bytes 475140 | tf_op jit(solution)/shard_map/while/body/eval_jaxpr/skr,krb->ksb/dot_general | solution.py:15
  74.6 1.6 %fusion.32 = f32[16,2,17,256]{3,2,1,0:T(8,128)S(1)} fusion(f32[16,2,17,256]{3,2,1,0:T(8,128)S(1)} %get-tuple-element.107, s32[]{:T(128)} %get-tuple-element.106, bf16[17,2,4096]{2,0,1:T(8,128)(2,1)S(1)} %get-tuple-element.114, s32[2,4096]{1,0:T(2,128)S(1)} %dynamic-slice_bitcast_fusion.2), kind=kOutput, calls=%fused_computation.6.clone.1 | convolution fusion | flops 73400320 | bytes 475140 | tf_op jit(solution)/shard_map/while/body/eval_jaxpr/skr,krb->ksb/dot_general | solution.py:15
  76.3 1.6 %fusion.32 = f32[16,2,17,256]{3,2,1,0:T(8,128)S(1)} fusion(f32[16,2,17,256]{3,2,1,0:T(8,128)S(1)} %get-tuple-element.107, s32[]{:T(128)} %get-tuple-element.106, bf16[17,2,4096]{2,0,1:T(8,128)(2,1)S(1)} %get-tuple-element.114, s32[2,4096]{1,0:T(2,128)S(1)} %dynamic-slice_bitcast_fusion.2), kind=kOutput, calls=%fused_computation.6.clone.1 | convolution fusion | flops 73400320 | bytes 475140 | tf_op jit(solution)/shard_map/while/body/eval_jaxpr/skr,krb->ksb/dot_general | solution.py:15
  78.0 1.6 %fusion.32 = f32[16,2,17,256]{3,2,1,0:T(8,128)S(1)} fusion(f32[16,2,17,256]{3,2,1,0:T(8,128)S(1)} %get-tuple-element.107, s32[]{:T(128)} %get-tuple-element.106, bf16[17,2,4096]{2,0,1:T(8,128)(2,1)S(1)} %get-tuple-element.114, s32[2,4096]{1,0:T(2,128)S(1)} %dynamic-slice_bitcast_fusion.2), kind=kOutput, calls=%fused_computation.6.clone.1 | convolution fusion | flops 73400320 | bytes 475140 | tf_op jit(solution)/shard_map/while/body/eval_jaxpr/skr,krb->ksb/dot_general | solution.py:15
  79.7 1.6 %fusion.32 = f32[16,2,17,256]{3,2,1,0:T(8,128)S(1)} fusion(f32[16,2,17,256]{3,2,1,0:T(8,128)S(1)} %get-tuple-element.107, s32[]{:T(128)} %get-tuple-element.106, bf16[17,2,4096]{2,0,1:T(8,128)(2,1)S(1)} %get-tuple-element.114, s32[2,4096]{1,0:T(2,128)S(1)} %dynamic-slice_bitcast_fusion.2), kind=kOutput, calls=%fused_computation.6.clone.1 | convolution fusion | flops 73400320 | bytes 475140 | tf_op jit(solution)/shard_map/while/body/eval_jaxpr/skr,krb->ksb/dot_general | solution.py:15
  81.3 1.6 %fusion.32 = f32[16,2,17,256]{3,2,1,0:T(8,128)S(1)} fusion(f32[16,2,17,256]{3,2,1,0:T(8,128)S(1)} %get-tuple-element.107, s32[]{:T(128)} %get-tuple-element.106, bf16[17,2,4096]{2,0,1:T(8,128)(2,1)S(1)} %get-tuple-element.114, s32[2,4096]{1,0:T(2,128)S(1)} %dynamic-slice_bitcast_fusion.2), kind=kOutput, calls=%fused_computation.6.clone.1 | convolution fusion | flops 73400320 | bytes 475140 | tf_op jit(solution)/shard_map/while/body/eval_jaxpr/skr,krb->ksb/dot_general | solution.py:15
  83.0 1.6 %fusion.32 = f32[16,2,17,256]{3,2,1,0:T(8,128)S(1)} fusion(f32[16,2,17,256]{3,2,1,0:T(8,128)S(1)} %get-tuple-element.107, s32[]{:T(128)} %get-tuple-element.106, bf16[17,2,4096]{2,0,1:T(8,128)(2,1)S(1)} %get-tuple-element.114, s32[2,4096]{1,0:T(2,128)S(1)} %dynamic-slice_bitcast_fusion.2), kind=kOutput, calls=%fused_computation.6.clone.1 | convolution fusion | flops 73400320 | bytes 475140 | tf_op jit(solution)/shard_map/while/body/eval_jaxpr/skr,krb->ksb/dot_general | solution.py:15
  84.7 1.6 %fusion.32 = f32[16,2,17,256]{3,2,1,0:T(8,128)S(1)} fusion(f32[16,2,17,256]{3,2,1,0:T(8,128)S(1)} %get-tuple-element.107, s32[]{:T(128)} %get-tuple-element.106, bf16[17,2,4096]{2,0,1:T(8,128)(2,1)S(1)} %get-tuple-element.114, s32[2,4096]{1,0:T(2,128)S(1)} %dynamic-slice_bitcast_fusion.2), kind=kOutput, calls=%fused_computation.6.clone.1 | convolution fusion | flops 73400320 | bytes 475140 | tf_op jit(solution)/shard_map/while/body/eval_jaxpr/skr,krb->ksb/dot_general | solution.py:15
  86.4 1.6 %fusion.32 = f32[16,2,17,256]{3,2,1,0:T(8,128)S(1)} fusion(f32[16,2,17,256]{3,2,1,0:T(8,128)S(1)} %get-tuple-element.107, s32[]{:T(128)} %get-tuple-element.106, bf16[17,2,4096]{2,0,1:T(8,128)(2,1)S(1)} %get-tuple-element.114, s32[2,4096]{1,0:T(2,128)S(1)} %dynamic-slice_bitcast_fusion.2), kind=kOutput, calls=%fused_computation.6.clone.1 | convolution fusion | flops 73400320 | bytes 475140 | tf_op jit(solution)/shard_map/while/body/eval_jaxpr/skr,krb->ksb/dot_general | solution.py:15
  88.1 1.6 %fusion.32 = f32[16,2,17,256]{3,2,1,0:T(8,128)S(1)} fusion(f32[16,2,17,256]{3,2,1,0:T(8,128)S(1)} %get-tuple-element.107, s32[]{:T(128)} %get-tuple-element.106, bf16[17,2,4096]{2,0,1:T(8,128)(2,1)S(1)} %get-tuple-element.114, s32[2,4096]{1,0:T(2,128)S(1)} %dynamic-slice_bitcast_fusion.2), kind=kOutput, calls=%fused_computation.6.clone.1 | convolution fusion | flops 73400320 | bytes 475140 | tf_op jit(solution)/shard_map/while/body/eval_jaxpr/skr,krb->ksb/dot_general | solution.py:15
  89.8 1.6 %fusion.32 = f32[16,2,17,256]{3,2,1,0:T(8,128)S(1)} fusion(f32[16,2,17,256]{3,2,1,0:T(8,128)S(1)} %get-tuple-element.107, s32[]{:T(128)} %get-tuple-element.106, bf16[17,2,4096]{2,0,1:T(8,128)(2,1)S(1)} %get-tuple-element.114, s32[2,4096]{1,0:T(2,128)S(1)} %dynamic-slice_bitcast_fusion.2), kind=kOutput, calls=%fused_computation.6.clone.1 | convolution fusion | flops 73400320 | bytes 475140 | tf_op jit(solution)/shard_map/while/body/eval_jaxpr/skr,krb->ksb/dot_general | solution.py:15
  91.4 1.6 %fusion.32 = f32[16,2,17,256]{3,2,1,0:T(8,128)S(1)} fusion(f32[16,2,17,256]{3,2,1,0:T(8,128)S(1)} %get-tuple-element.107, s32[]{:T(128)} %get-tuple-element.106, bf16[17,2,4096]{2,0,1:T(8,128)(2,1)S(1)} %get-tuple-element.114, s32[2,4096]{1,0:T(2,128)S(1)} %dynamic-slice_bitcast_fusion.2), kind=kOutput, calls=%fused_computation.6.clone.1 | convolution fusion | flops 73400320 | bytes 475140 | tf_op jit(solution)/shard_map/while/body/eval_jaxpr/skr,krb->ksb/dot_general | solution.py:15
  93.1 1.6 %fusion.32 = f32[16,2,17,256]{3,2,1,0:T(8,128)S(1)} fusion(f32[16,2,17,256]{3,2,1,0:T(8,128)S(1)} %get-tuple-element.107, s32[]{:T(128)} %get-tuple-element.106, bf16[17,2,4096]{2,0,1:T(8,128)(2,1)S(1)} %get-tuple-element.114, s32[2,4096]{1,0:T(2,128)S(1)} %dynamic-slice_bitcast_fusion.2), kind=kOutput, calls=%fused_computation.6.clone.1 | convolution fusion | flops 73400320 | bytes 475140 | tf_op jit(solution)/shard_map/while/body/eval_jaxpr/skr,krb->ksb/dot_general | solution.py:15
  94.8 1.6 %fusion.32 = f32[16,2,17,256]{3,2,1,0:T(8,128)S(1)} fusion(f32[16,2,17,256]{3,2,1,0:T(8,128)S(1)} %get-tuple-element.107, s32[]{:T(128)} %get-tuple-element.106, bf16[17,2,4096]{2,0,1:T(8,128)(2,1)S(1)} %get-tuple-element.114, s32[2,4096]{1,0:T(2,128)S(1)} %dynamic-slice_bitcast_fusion.2), kind=kOutput, calls=%fused_computation.6.clone.1 | convolution fusion | flops 73400320 | bytes 475140 | tf_op jit(solution)/shard_map/while/body/eval_jaxpr/skr,krb->ksb/dot_general | solution.py:15
  96.5 0.5 fusion.8
  97.0 0.3 slice_reduce_fusion.1
  97.3 0.2 broadcast_subtract_fusion
  97.5 0.3 fusion.10
  97.8 0.4 fusion.13
  98.2 0.4 fusion.23
  98.7 0.2 fusion.22
  98.8 0.6 broadcast_in_dim.13
  99.4 6.8 %all-to-all-start.1 = ((f32[16,1,2]{2,1,0:T(1,128)}), f32[16,1,2]{2,1,0:T(1,128)S(1)}, u32[]{:S(2)}, u32[]{:S(2)}) async-start(f32[16,1,2]{2,1,0:T(1,128)} %broadcast_in_dim.13), calls=%async_computation.1 | async-start | bytes 16384 | tf_op jit(solution)/shard_map/all_to_all | solution.py:77
  106.2 1.1 copy.96
  107.3 5.3 %all-to-all-done.1 = f32[16,1,2]{2,1,0:T(1,128)S(1)} async-done(((f32[16,1,2]{2,1,0:T(1,128)}), f32[16,1,2]{2,1,0:T(1,128)S(1)}, u32[]{:S(2)}, u32[]{:S(2)}) %all-to-all-start.1) | async-done | bytes 160 | tf_op jit(solution)/shard_map/all_to_all | solution.py:77
  112.6 0.5 reduce_max.19
  (32 shorter events, 0.3 us)
Async XLA Ops:
  0.6 2.3 %copy-start.2 = (s32[4096]{0:T(1024)S(1)}, s32[4096]{0:T(1024)}, u32[]{:S(2)}) copy-start(s32[4096]{0:T(1024)} %param.9) | copy-start | bytes 49156
  0.6 2.3 %copy-start.1 = (bf16[16,4096]{1,0:T(8,128)(2,1)S(1)}, bf16[16,4096]{1,0:T(8,128)(2,1)}, u32[]{:S(2)}) copy-start(bf16[16,4096]{1,0:T(8,128)(2,1)} %param.8) | copy-start | bytes 393220
  0.7 2.4 %copy-start = (bf16[16,4096]{1,0:T(8,128)(2,1)S(1)}, bf16[16,4096]{1,0:T(8,128)(2,1)}, u32[]{:S(2)}) copy-start(bf16[16,4096]{1,0:T(8,128)(2,1)} %param.7) | copy-start | bytes 393220
  17.8 50.9 %all-to-all-start = ((bf16[33,32,2,128]{3,2,0,1:T(2,128)(2,1)}), bf16[33,32,2,128]{3,2,0,1:T(2,128)(2,1)S(1)}, u32[]{:S(2)}, u32[]{:S(2)}) async-start(bf16[33,32,2,128]{3,2,0,1:T(2,128)(2,1)} %copy.61), calls=%async_computation | async-start | bytes 1081344 | tf_op jit(solution)/shard_map/all_to_all | solution.py:61
  99.4 13.2 %all-to-all-start.1 = ((f32[16,1,2]{2,1,0:T(1,128)}), f32[16,1,2]{2,1,0:T(1,128)S(1)}, u32[]{:S(2)}, u32[]{:S(2)}) async-start(f32[16,1,2]{2,1,0:T(1,128)} %broadcast_in_dim.13), calls=%async_computation.1 | async-start | bytes 16384 | tf_op jit(solution)/shard_map/all_to_all | solution.py:77

commit v2 on v1

--- a/solution.py
+++ b/solution.py
@@ -8,14 +8,9 @@
 
 
 def feature_histograms(bin_table, statistics):
-    levels = lax.broadcasted_iota(jnp.int32, (1, 1, B), 2)
-
-    def one_feature(bin_row):
-        indicator = (bin_row[:, :, None] == levels).astype(jnp.bfloat16)
-        return jnp.einsum("skr,krb->ksb", statistics, indicator, preferred_element_type=jnp.float32)
-
-    stacked = lax.map(one_feature, bin_table)
-    return jnp.transpose(stacked, (1, 0, 2, 3))
+    levels = lax.broadcasted_iota(jnp.int32, (1, 1, 1, B), 3)
+    indicator = (bin_table[:, :, :, None] == levels).astype(jnp.bfloat16)
+    return jnp.einsum("skr,fkrb->kfsb", statistics, indicator, preferred_element_type=jnp.float32)
 
 
 def running_rank(owned):
@@ -58,10 +53,18 @@
         jnp.zeros((payload_width, node_total * capacity), jnp.bfloat16).at[:, position].set(payload)
     )
     outgoing = outgoing.reshape(payload_width, node_devices, node_local, capacity)
-    arrived = lax.all_to_all(outgoing, "node", split_axis=1, concat_axis=3, tiled=True)[:, 0]
-    bin_table = jnp.floor(arrived[:feat_count].astype(jnp.float32) * B).astype(jnp.int32)
-    statistics = arrived[feat_count:]
-    histogram = feature_histograms(bin_table, statistics)
+    half = feat_count // 2
+    first = jnp.concatenate([outgoing[feat_count:], outgoing[:half]], axis=0)
+    second = outgoing[half:feat_count]
+    stat_count = payload_width - feat_count
+    arrived_a = lax.all_to_all(first, "node", split_axis=1, concat_axis=3, tiled=True)[:, 0]
+    arrived_b = lax.all_to_all(second, "node", split_axis=1, concat_axis=3, tiled=True)[:, 0]
+    statistics = arrived_a[:stat_count]
+    bins_a = jnp.floor(arrived_a[stat_count:].astype(jnp.float32) * B).astype(jnp.int32)
+    hist_a = feature_histograms(bins_a, statistics)
+    bins_b = jnp.floor(arrived_b.astype(jnp.float32) * B).astype(jnp.int32)
+    hist_b = feature_histograms(bins_b, statistics)
+    histogram = jnp.concatenate([hist_a, hist_b], axis=1)
     c = lax.broadcasted_iota(jnp.int32, (B, B), 0)
     b = lax.broadcasted_iota(jnp.int32, (B, B), 1)
     upper = (c <= b).astype(jnp.float32)

time: 113 us -> 135 us (1.19)
  local copies, waits for them, and re-layouts: 18 us -> 26.4 us
  starting transfers between devices: 23.5 us -> 28.7 us
  matrix products: 27.3 us -> 31.6 us
  waiting for transfers between devices: 39.5 us -> 42.2 us
    slice x2 -> x7, local copies, waits for them, and re-layouts: 0.09 us -> 11.3 us  [the longest x4 8.72 us: on_device(): first = jnp.concatenate([outgoing[feat_count:], outgoing[:half]], axis=0)]
    all_to_all x1 -> x2, starting transfers between devices: 16.7 us -> 21.9 us  [the longest x1 16.8 us: on_device(): lax.all_to_all(second, 'node', split_axis=1, concat_axis=3, tiled=True)]
    dot_general x16 -> x2, matrix products: 26.3 us -> 30.7 us  [feature_histograms(): jnp.einsum('skr,fkrb->kfsb', statistics, indicator, preferred_element_typ...]
    reshape x1 -> x0, local copies, waits for them, and re-layouts: 2.62 us -> none  [on_device(): outgoing.reshape(payload_width, node_devices, node_local, capacity)]
    all_to_all x1 -> x2, waiting for transfers between devices: 34.2 us -> 36.8 us  [the longest x1 28.5 us: on_device(): lax.all_to_all(first, 'node', split_axis=1, concat_axis=3, tiled=True)[:, 0]]
  transfers between devices with their start and end apart: 2 -> 3, of which waited for: 2 -> 3; matrix products, arithmetic and copies ran while one was open for 1% -> 6% of each run, Pallas kernels for 0% -> 0%
where the time goes in v2:
time: 135 us
  waiting for transfers between devices  42.2 us (31%)
  matrix products  31.6 us (23%)
  starting transfers between devices  28.7 us (21%)
  local copies, waits for them, and re-layouts  26.4 us (20%)
  other arithmetic  4.91 us (4%)
    dot_general x2, matrix products, feature_histograms(): jnp.einsum('skr,fkrb->kfsb', statistics, indicator, preferred_element_typ...  30.7 us
    all_to_all x1, waiting for transfers between devices, on_device(): lax.all_to_all(first, 'node', split_axis=1, concat_axis=3, tiled=True)[:, 0]  28.5 us
    all_to_all x1, starting transfers between devices, on_device(): lax.all_to_all(second, 'node', split_axis=1, concat_axis=3, tiled=True)  16.8 us
    scatter x1, local copies, waits for them, and re-layouts, on_device(): jnp.zeros((payload_width, node_total * capacity), jnp.bfloat16)  11.6 us
    slice x4, local copies, waits for them, and re-layouts, on_device(): first = jnp.concatenate([outgoing[feat_count:], outgoing[:half]], axis=0)  8.72 us
    all_to_all x1, waiting for transfers between devices, on_device(): lax.all_to_all(second, 'node', split_axis=1, concat_axis=3, tiled=True)  8.31 us
    all_to_all x1, starting transfers between devices, on_device(): lax.all_to_all(spread, 'feat', split_axis=0, concat_axis=0, tiled=True)  6.75 us
    all_to_all x1, waiting for transfers between devices, on_device(): lax.all_to_all(spread, 'feat', split_axis=0, concat_axis=0, tiled=True)  5.37 us
  transfers between devices with their start and end apart: 3, of which 3 were waited for; matrix products, arithmetic and copies ran while one was open for 6% of the time, Pallas kernels for 0%

profile of v2, /device:TPU:1, one launch (start us, length us, event | category | flops | bytes accessed | tf_op | source)
XLA Modules:
  0.0 134.7 jit_solution(18150748646480493767)
XLA Ops:
  0.6 0.0 copy-start.3
  0.6 0.0 copy-start.2
  0.7 0.0 copy-start.1
  0.7 1.0 select_reduce_fusion
  1.7 0.3 convolution_bitcast_fusion
  2.0 0.4 slice_reduce_fusion
  2.4 0.1 fusion.25
  2.6 0.3 multiply_reduce_fusion
  2.9 0.0 copy-done.3
  3.0 0.0 copy-done.2
  3.0 0.0 copy-done.1
  3.0 0.1 maximum_bitcast_fusion
  3.1 0.5 copy.71
  3.6 11.6 %scatter_custom_fusion = bf16[33,8192]{0,1:T(8,128)(2,1)S(1)} fusion(s32[4096]{0:T(1024)S(1)} %bitcast.73, bf16[4096,33]{1,0:T(8,128)(2,1)S(1)} %copy.71, bf16[]{:T(256)} %constant.10.clone.1), kind=kCustom, calls=%fused_computation.15 | custom fusion | bytes 540674 | tf_op jit(solution)/shard_map/scatter | solution.py:53
  15.2 2.7 %fusion.27 = (bf16[8,8192]{0,1:T(8,128)(2,1)}, bf16[8,8192]{0,1:T(8,128)(2,1)}) fusion(bf16[33,8192]{0,1:T(8,128)(2,1)S(1)} %scatter_custom_fusion), kind=kLoop, calls=%fused_computation.58 | loop fusion | bytes 524288 | tf_op jit(solution)/shard_map/slice | solution.py:57
  17.9 2.5 %copy.77 = bf16[8,32,2,128]{3,0,2,1:T(8,128)(2,1)} copy(bf16[8,32,2,128]{0,3,2,1:T(8,128)(2,1)} %bitcast.66) | data formatting | bytes 262144 | tf_op jit(solution)/shard_map/slice | solution.py:58
  20.3 16.8 %all-to-all-start.1 = ((bf16[8,32,2,128]{3,0,2,1:T(8,128)(2,1)}), bf16[8,32,2,128]{3,0,2,1:T(8,128)(2,1)S(1)}, u32[]{:S(2)}, u32[]{:S(2)}) async-start(bf16[8,32,2,128]{3,0,2,1:T(8,128)(2,1)} %copy.77), calls=%async_computation.1 | async-start | bytes 262144 | tf_op jit(solution)/shard_map/all_to_all | solution.py:61
  37.1 1.9 %slice.75 = bf16[17,8192]{0,1:T(8,128)(2,1)} slice(bf16[33,8192]{0,1:T(8,128)(2,1)S(1)} %scatter_custom_fusion), slice={[16:33], [0:8192]} | slice | bytes 557056 | tf_op jit(solution)/shard_map/slice | solution.py:57
  39.0 0.0 copy-start
  39.0 2.0 %copy.73 = bf16[8,32,2,128]{3,2,0,1:T(2,128)(2,1)S(1)} copy(bf16[8,32,2,128]{0,3,2,1:T(8,128)(2,1)} %bitcast.65) | data formatting | bytes 262144 | tf_op jit(solution)/shard_map/slice | solution.py:57
  41.0 0.2 copy-done
  41.2 2.1 %copy.72 = bf16[17,32,2,128]{3,2,0,1:T(2,128)(2,1)S(1)} copy(bf16[17,32,2,128]{0,3,2,1:T(8,128)(2,1)S(1)} %bitcast.64) | data formatting | bytes 557056 | tf_op jit(solution)/shard_map/slice | solution.py:57
  43.3 1.3 pad_maximum_fusion.1
  44.6 8.3 %all-to-all-done.1 = bf16[8,32,2,128]{3,0,2,1:T(8,128)(2,1)S(1)} async-done(((bf16[8,32,2,128]{3,0,2,1:T(8,128)(2,1)}), bf16[8,32,2,128]{3,0,2,1:T(8,128)(2,1)S(1)}, u32[]{:S(2)}, u32[]{:S(2)}) %all-to-all-start.1) | async-done | bytes 131104 | tf_op jit(solution)/shard_map/all_to_all | solution.py:61
  52.9 5.1 %all-to-all-start = ((bf16[25,32,2,128]{3,2,0,1:T(2,128)(2,1)}), bf16[25,32,2,128]{3,2,0,1:T(2,128)(2,1)S(1)}, u32[]{:S(2)}, u32[]{:S(2)}) async-start(bf16[25,32,2,128]{3,2,0,1:T(2,128)(2,1)} %pad_maximum_fusion.1), calls=%async_computation | async-start | bytes 819200 | tf_op jit(solution)/shard_map/all_to_all | solution.py:60
  58.1 0.1 copy.78
  58.2 0.1 convert_element_type.94
  58.3 28.5 %all-to-all-done = bf16[25,32,2,128]{3,2,0,1:T(2,128)(2,1)S(1)} async-done(((bf16[25,32,2,128]{3,2,0,1:T(2,128)(2,1)}), bf16[25,32,2,128]{3,2,0,1:T(2,128)(2,1)S(1)}, u32[]{:S(2)}, u32[]{:S(2)}) %all-to-all-start) | async-done | bytes 409632 | tf_op jit(solution)/shard_map/all_to_all | solution.py:60
  86.8 0.1 copy.116
  87.0 0.1 slice.64
  87.0 0.1 reshape.131
  87.2 0.2 copy.87
  87.4 15.3 %fusion.5 = f32[2,8,17,256]{3,2,1,0:T(8,128)S(1)} fusion(s32[8,2,4096]{2,0,1:T(8,128)S(1)} %copy.87, bf16[17,2,4096,1]{2,1,0,3:T(2,128)(2,1)S(1)} %bitcast.69), kind=kOutput, calls=%fused_computation.9 | convolution fusion | flops 587202560 | bytes 819200 | tf_op jit(solution)/shard_map/skr,fkrb->kfsb/dot_general | solution.py:13
  102.7 15.3 %fusion.4 = f32[2,8,17,256]{3,2,1,0:T(8,128)S(1)} fusion(s32[8,2,4096]{2,0,1:T(8,128)S(1)} %convert_element_type.94, bf16[17,2,4096,1]{2,1,0,3:T(2,128)(2,1)S(1)} %bitcast.70), kind=kOutput, calls=%fused_computation.8 | convolution fusion | flops 587202560 | bytes 819200 | tf_op jit(solution)/shard_map/skr,fkrb->kfsb/dot_general | solution.py:13
  118.1 0.5 fusion.17
  118.6 0.4 fusion.13
  119.0 0.4 fusion.24
  119.4 0.3 slice_reduce_fusion.1
  119.7 0.2 broadcast_subtract_fusion
  119.9 0.3 fusion.8
  120.3 0.2 fusion.23
  120.4 0.6 broadcast_in_dim.5
  121.0 6.8 %all-to-all-start.2 = ((f32[16,1,2]{2,1,0:T(1,128)}), f32[16,1,2]{2,1,0:T(1,128)S(1)}, u32[]{:S(2)}, u32[]{:S(2)}) async-start(f32[16,1,2]{2,1,0:T(1,128)} %broadcast_in_dim.5), calls=%async_computation.2 | async-start | bytes 16384 | tf_op jit(solution)/shard_map/all_to_all | solution.py:80
  127.8 0.1 pad_maximum_fusion
  127.9 1.0 copy.83
  128.8 5.4 %all-to-all-done.2 = f32[16,1,2]{2,1,0:T(1,128)S(1)} async-done(((f32[16,1,2]{2,1,0:T(1,128)}), f32[16,1,2]{2,1,0:T(1,128)S(1)}, u32[]{:S(2)}, u32[]{:S(2)}) %all-to-all-start.2) | async-done | bytes 160 | tf_op jit(solution)/shard_map/all_to_all | solution.py:80
  134.2 0.5 reduce_max.19
  (14 shorter events, 0.3 us)
Async XLA Ops:
  0.6 2.3 %copy-start.3 = (s32[4096]{0:T(1024)S(1)}, s32[4096]{0:T(1024)}, u32[]{:S(2)}) copy-start(s32[4096]{0:T(1024)} %param.7) | copy-start | bytes 49156
  0.6 2.3 %copy-start.2 = (bf16[16,4096]{1,0:T(8,128)(2,1)S(1)}, bf16[16,4096]{1,0:T(8,128)(2,1)}, u32[]{:S(2)}) copy-start(bf16[16,4096]{1,0:T(8,128)(2,1)} %param.6) | copy-start | bytes 393220
  0.7 2.4 %copy-start.1 = (bf16[16,4096]{1,0:T(8,128)(2,1)S(1)}, bf16[16,4096]{1,0:T(8,128)(2,1)}, u32[]{:S(2)}) copy-start(bf16[16,4096]{1,0:T(8,128)(2,1)} %param.5) | copy-start | bytes 393220
  20.3 32.6 %all-to-all-start.1 = ((bf16[8,32,2,128]{3,0,2,1:T(8,128)(2,1)}), bf16[8,32,2,128]{3,0,2,1:T(8,128)(2,1)S(1)}, u32[]{:S(2)}, u32[]{:S(2)}) async-start(bf16[8,32,2,128]{3,0,2,1:T(8,128)(2,1)} %copy.77), calls=%async_computation.1 | async-start | bytes 262144 | tf_op jit(solution)/shard_map/all_to_all | solution.py:61
  39.0 2.2 %copy-start = (bf16[17,8192]{0,1:T(8,128)(2,1)S(1)}, bf16[17,8192]{0,1:T(8,128)(2,1)}, u32[]{:S(2)}) copy-start(bf16[17,8192]{0,1:T(8,128)(2,1)} %slice.75) | copy-start | bytes 835588
  52.9 33.9 %all-to-all-start = ((bf16[25,32,2,128]{3,2,0,1:T(2,128)(2,1)}), bf16[25,32,2,128]{3,2,0,1:T(2,128)(2,1)S(1)}, u32[]{:S(2)}, u32[]{:S(2)}) async-start(bf16[25,32,2,128]{3,2,0,1:T(2,128)(2,1)} %pad_maximum_fusion.1), calls=%async_computation | async-start | bytes 819200 | tf_op jit(solution)/shard_map/all_to_all | solution.py:60
  121.0 13.2 %all-to-all-start.2 = ((f32[16,1,2]{2,1,0:T(1,128)}), f32[16,1,2]{2,1,0:T(1,128)S(1)}, u32[]{:S(2)}, u32[]{:S(2)}) async-start(f32[16,1,2]{2,1,0:T(1,128)} %broadcast_in_dim.5), calls=%async_computation.2 | async-start | bytes 16384 | tf_op jit(solution)/shard_map/all_to_all | solution.py:80

commit v3 on v1

--- a/solution.py
+++ b/solution.py
@@ -43,24 +43,25 @@
     node_total = node_slot.shape[0]
     node_local = node_total // node_devices
     capacity = 2 * row_count // node_total
-    weight = (1 - honest).astype(jnp.float32)
+    kept = honest == 0
     columns = lax.broadcasted_iota(jnp.int32, (1, node_total), 1)
     named = (destination == columns).astype(jnp.int32)
     target = jnp.sum(named * node_slot[None, :], axis=1)
-    owned = (target[:, None] == columns).astype(jnp.int32)
+    owned = ((target[:, None] == columns) & kept[:, None]).astype(jnp.int32)
     rank = running_rank(owned)
-    position = target * capacity + rank
-    weighted = weight[None, :] * pseudo.astype(jnp.float32)
-    weight_row = weight[None, :].astype(jnp.bfloat16)
-    payload = jnp.concatenate([covariates, weight_row, weighted.astype(jnp.bfloat16)], axis=0)
+    slots = node_total * capacity
+    position = jnp.where(kept, target * capacity + rank, slots)
+    payload = jnp.concatenate([covariates, pseudo], axis=0)
     payload_width = payload.shape[0]
-    outgoing = (
-        jnp.zeros((payload_width, node_total * capacity), jnp.bfloat16).at[:, position].set(payload)
+    empty = jnp.concatenate(
+        [jnp.ones((feat_count, slots), jnp.bfloat16), jnp.zeros((payload_width - feat_count, slots), jnp.bfloat16)]
     )
+    outgoing = empty.at[:, position].set(payload, mode="drop")
     outgoing = outgoing.reshape(payload_width, node_devices, node_local, capacity)
     arrived = lax.all_to_all(outgoing, "node", split_axis=1, concat_axis=3, tiled=True)[:, 0]
     bin_table = jnp.floor(arrived[:feat_count].astype(jnp.float32) * B).astype(jnp.int32)
-    statistics = arrived[feat_count:]
+    ones = jnp.ones((1,) + arrived.shape[1:], jnp.bfloat16)
+    statistics = jnp.concatenate([ones, arrived[feat_count:]], axis=0)
     histogram = feature_histograms(bin_table, statistics)
     c = lax.broadcasted_iota(jnp.int32, (B, B), 0)
     b = lax.broadcasted_iota(jnp.int32, (B, B), 1)

time: 113 us -> 114 us (level)
  no operation moved by 1% of the time
where the time goes in v3:
time: 114 us; the launch traced here: 113 us
  waiting for transfers between devices  38.8 us (34%)
  matrix products  27.3 us (24%)
  starting transfers between devices  23.5 us (21%)
  local copies, waits for them, and re-layouts  17.8 us (16%)
  other arithmetic  4.27 us (4%)
    all_to_all x1, waiting for transfers between devices, on_device(): lax.all_to_all(outgoing, 'node', split_axis=1, concat_axis=3, tiled=True)  33.5 us
    dot_general x16, matrix products, one_feature(): jnp.einsum('skr,krb->ksb', statistics, indicator, preferred_element_type=...  26.3 us
    all_to_all x1, starting transfers between devices, on_device(): lax.all_to_all(outgoing, 'node', split_axis=1, concat_axis=3, tiled=True)  16.7 us
    scatter x1, local copies, waits for them, and re-layouts, on_device(): outgoing = empty.at[:, position].set(payload, mode='drop')  12 us
    all_to_all x1, starting transfers between devices, on_device(): lax.all_to_all(spread, 'feat', split_axis=0, concat_axis=0, tiled=True)  6.76 us
    all_to_all x1, waiting for transfers between devices, on_device(): lax.all_to_all(spread, 'feat', split_axis=0, concat_axis=0, tiled=True)  5.27 us
  transfers between devices with their start and end apart: 2, of which 2 were waited for; matrix products, arithmetic and copies ran while one was open for 1% of the time, Pallas kernels for 0%

profile of v3, /device:TPU:1, one launch (start us, length us, event | category | flops | bytes accessed | tf_op | source)
XLA Modules:
  0.0 113.0 jit_solution(109495407778569559)
XLA Ops:
  0.6 0.0 copy-start.2
  0.7 1.0 select_reduce_fusion
  1.7 0.7 broadcast_compare_fusion
  2.4 0.4 convolution_bitcast_fusion
  2.8 0.4 slice_reduce_fusion
  3.2 0.1 fusion.24
  3.3 0.4 multiply_reduce_fusion
  3.8 0.5 copy.45
  4.3 0.3 concatenate.12
  4.6 12.0 %scatter_fusion = bf16[32,8192]{0,1:T(8,128)(2,1)S(1)} fusion(bf16[32,8192]{0,1:T(8,128)(2,1)S(1)} %concatenate.12, s32[4096]{0:T(1024)S(1)} %compare_select_fusion, bf16[4096,32]{1,0:T(8,128)(2,1)S(1)} %copy.45), kind=kCustom, calls=%fused_computation | custom fusion | bytes 802816 | tf_op jit(solution)/shard_map/scatter | solution.py:59
  16.6 1.5 %copy.46 = bf16[32,32,2,128]{3,0,2,1:T(8,128)(2,1)} copy(bf16[32,32,2,128]{0,3,2,1:T(8,128)(2,1)S(1)} %bitcast.67) | data formatting | bytes 1048576 | tf_op jit(solution)/shard_map/reshape | solution.py:60
  18.1 16.7 %all-to-all-start = ((bf16[32,32,2,128]{3,0,2,1:T(8,128)(2,1)}), bf16[32,32,2,128]{3,0,2,1:T(8,128)(2,1)S(1)}, u32[]{:S(2)}, u32[]{:S(2)}) async-start(bf16[32,32,2,128]{3,0,2,1:T(8,128)(2,1)} %copy.46), calls=%async_computation | async-start | bytes 1048576 | tf_op jit(solution)/shard_map/all_to_all | solution.py:61
  34.8 33.5 %all-to-all-done = bf16[32,32,2,128]{3,0,2,1:T(8,128)(2,1)S(1)} async-done(((bf16[32,32,2,128]{3,0,2,1:T(8,128)(2,1)}), bf16[32,32,2,128]{3,0,2,1:T(8,128)(2,1)S(1)}, u32[]{:S(2)}, u32[]{:S(2)}) %all-to-all-start) | async-done | bytes 524320 | tf_op jit(solution)/shard_map/all_to_all | solution.py:61
  68.3 0.1 floor_convert_fusion
  68.5 0.3 copy.56
  68.8 0.3 reshape.75
  69.1 0.1 copy.48
  69.2 0.1 slice.42
  69.3 0.1 concatenate.14
  69.4 26.9 %while.11 = (s32[]{:T(128)}, f32[16,2,17,256]{3,2,1,0:T(8,128)S(1)}, s32[16,2,4096]{2,1,0:T(2,128)S(1)}, bf16[17,2,4096]{2,0,1:T(8,128)(2,1)S(1)}, s32[]{:T(128)}) while((s32[]{:T(128)}, f32[16,2,17,256]{3,2,1,0:T(8,128)S(1)}, s32[16,2,4096]{2,1,0:T(2,128)S(1)}, bf16[17,2,4096]{2,0,1:T(8,128)(2,1)S(1)}, s32[]{:T(128)}) %tuple.29), condition=%wide.region_4.5_spmd.clone, body=%wide.region_3.4_spmd.clone.sunk | while | flops 73400320 | bytes 540741 | solution.py:17
  69.4 1.6 %fusion.31 = f32[16,2,17,256]{3,2,1,0:T(8,128)S(1)} fusion(f32[16,2,17,256]{3,2,1,0:T(8,128)S(1)} %get-tuple-element.93, s32[]{:T(128)} %get-tuple-element.92, bf16[17,2,4096]{2,0,1:T(8,128)(2,1)S(1)} %get-tuple-element.100, s32[2,4096]{1,0:T(2,128)S(1)} %dynamic-slice_bitcast_fusion.2), kind=kOutput, calls=%fused_computation.6.clone.1 | convolution fusion | flops 73400320 | bytes 475140 | tf_op jit(solution)/shard_map/while/body/eval_jaxpr/skr,krb->ksb/dot_general | solution.py:15
  71.1 1.6 %fusion.31 = f32[16,2,17,256]{3,2,1,0:T(8,128)S(1)} fusion(f32[16,2,17,256]{3,2,1,0:T(8,128)S(1)} %get-tuple-element.93, s32[]{:T(128)} %get-tuple-element.92, bf16[17,2,4096]{2,0,1:T(8,128)(2,1)S(1)} %get-tuple-element.100, s32[2,4096]{1,0:T(2,128)S(1)} %dynamic-slice_bitcast_fusion.2), kind=kOutput, calls=%fused_computation.6.clone.1 | convolution fusion | flops 73400320 | bytes 475140 | tf_op jit(solution)/shard_map/while/body/eval_jaxpr/skr,krb->ksb/dot_general | solution.py:15
  72.8 1.6 %fusion.31 = f32[16,2,17,256]{3,2,1,0:T(8,128)S(1)} fusion(f32[16,2,17,256]{3,2,1,0:T(8,128)S(1)} %get-tuple-element.93, s32[]{:T(128)} %get-tuple-element.92, bf16[17,2,4096]{2,0,1:T(8,128)(2,1)S(1)} %get-tuple-element.100, s32[2,4096]{1,0:T(2,128)S(1)} %dynamic-slice_bitcast_fusion.2), kind=kOutput, calls=%fused_computation.6.clone.1 | convolution fusion | flops 73400320 | bytes 475140 | tf_op jit(solution)/shard_map/while/body/eval_jaxpr/skr,krb->ksb/dot_general | solution.py:15
  74.5 1.6 %fusion.31 = f32[16,2,17,256]{3,2,1,0:T(8,128)S(1)} fusion(f32[16,2,17,256]{3,2,1,0:T(8,128)S(1)} %get-tuple-element.93, s32[]{:T(128)} %get-tuple-element.92, bf16[17,2,4096]{2,0,1:T(8,128)(2,1)S(1)} %get-tuple-element.100, s32[2,4096]{1,0:T(2,128)S(1)} %dynamic-slice_bitcast_fusion.2), kind=kOutput, calls=%fused_computation.6.clone.1 | convolution fusion | flops 73400320 | bytes 475140 | tf_op jit(solution)/shard_map/while/body/eval_jaxpr/skr,krb->ksb/dot_general | solution.py:15
  76.2 1.6 %fusion.31 = f32[16,2,17,256]{3,2,1,0:T(8,128)S(1)} fusion(f32[16,2,17,256]{3,2,1,0:T(8,128)S(1)} %get-tuple-element.93, s32[]{:T(128)} %get-tuple-element.92, bf16[17,2,4096]{2,0,1:T(8,128)(2,1)S(1)} %get-tuple-element.100, s32[2,4096]{1,0:T(2,128)S(1)} %dynamic-slice_bitcast_fusion.2), kind=kOutput, calls=%fused_computation.6.clone.1 | convolution fusion | flops 73400320 | bytes 475140 | tf_op jit(solution)/shard_map/while/body/eval_jaxpr/skr,krb->ksb/dot_general | solution.py:15
  77.8 1.6 %fusion.31 = f32[16,2,17,256]{3,2,1,0:T(8,128)S(1)} fusion(f32[16,2,17,256]{3,2,1,0:T(8,128)S(1)} %get-tuple-element.93, s32[]{:T(128)} %get-tuple-element.92, bf16[17,2,4096]{2,0,1:T(8,128)(2,1)S(1)} %get-tuple-element.100, s32[2,4096]{1,0:T(2,128)S(1)} %dynamic-slice_bitcast_fusion.2), kind=kOutput, calls=%fused_computation.6.clone.1 | convolution fusion | flops 73400320 | bytes 475140 | tf_op jit(solution)/shard_map/while/body/eval_jaxpr/skr,krb->ksb/dot_general | solution.py:15
  79.5 1.6 %fusion.31 = f32[16,2,17,256]{3,2,1,0:T(8,128)S(1)} fusion(f32[16,2,17,256]{3,2,1,0:T(8,128)S(1)} %get-tuple-element.93, s32[]{:T(128)} %get-tuple-element.92, bf16[17,2,4096]{2,0,1:T(8,128)(2,1)S(1)} %get-tuple-element.100, s32[2,4096]{1,0:T(2,128)S(1)} %dynamic-slice_bitcast_fusion.2), kind=kOutput, calls=%fused_computation.6.clone.1 | convolution fusion | flops 73400320 | bytes 475140 | tf_op jit(solution)/shard_map/while/body/eval_jaxpr/skr,krb->ksb/dot_general | solution.py:15
  81.2 1.6 %fusion.31 = f32[16,2,17,256]{3,2,1,0:T(8,128)S(1)} fusion(f32[16,2,17,256]{3,2,1,0:T(8,128)S(1)} %get-tuple-element.93, s32[]{:T(128)} %get-tuple-element.92, bf16[17,2,4096]{2,0,1:T(8,128)(2,1)S(1)} %get-tuple-element.100, s32[2,4096]{1,0:T(2,128)S(1)} %dynamic-slice_bitcast_fusion.2), kind=kOutput, calls=%fused_computation.6.clone.1 | convolution fusion | flops 73400320 | bytes 475140 | tf_op jit(solution)/shard_map/while/body/eval_jaxpr/skr,krb->ksb/dot_general | solution.py:15
  82.9 1.6 %fusion.31 = f32[16,2,17,256]{3,2,1,0:T(8,128)S(1)} fusion(f32[16,2,17,256]{3,2,1,0:T(8,128)S(1)} %get-tuple-element.93, s32[]{:T(128)} %get-tuple-element.92, bf16[17,2,4096]{2,0,1:T(8,128)(2,1)S(1)} %get-tuple-element.100, s32[2,4096]{1,0:T(2,128)S(1)} %dynamic-slice_bitcast_fusion.2), kind=kOutput, calls=%fused_computation.6.clone.1 | convolution fusion | flops 73400320 | bytes 475140 | tf_op jit(solution)/shard_map/while/body/eval_jaxpr/skr,krb->ksb/dot_general | solution.py:15
  84.6 1.6 %fusion.31 = f32[16,2,17,256]{3,2,1,0:T(8,128)S(1)} fusion(f32[16,2,17,256]{3,2,1,0:T(8,128)S(1)} %get-tuple-element.93, s32[]{:T(128)} %get-tuple-element.92, bf16[17,2,4096]{2,0,1:T(8,128)(2,1)S(1)} %get-tuple-element.100, s32[2,4096]{1,0:T(2,128)S(1)} %dynamic-slice_bitcast_fusion.2), kind=kOutput, calls=%fused_computation.6.clone.1 | convolution fusion | flops 73400320 | bytes 475140 | tf_op jit(solution)/shard_map/while/body/eval_jaxpr/skr,krb->ksb/dot_general | solution.py:15
  86.3 1.6 %fusion.31 = f32[16,2,17,256]{3,2,1,0:T(8,128)S(1)} fusion(f32[16,2,17,256]{3,2,1,0:T(8,128)S(1)} %get-tuple-element.93, s32[]{:T(128)} %get-tuple-element.92, bf16[17,2,4096]{2,0,1:T(8,128)(2,1)S(1)} %get-tuple-element.100, s32[2,4096]{1,0:T(2,128)S(1)} %dynamic-slice_bitcast_fusion.2), kind=kOutput, calls=%fused_computation.6.clone.1 | convolution fusion | flops 73400320 | bytes 475140 | tf_op jit(solution)/shard_map/while/body/eval_jaxpr/skr,krb->ksb/dot_general | solution.py:15
  87.9 1.6 %fusion.31 = f32[16,2,17,256]{3,2,1,0:T(8,128)S(1)} fusion(f32[16,2,17,256]{3,2,1,0:T(8,128)S(1)} %get-tuple-element.93, s32[]{:T(128)} %get-tuple-element.92, bf16[17,2,4096]{2,0,1:T(8,128)(2,1)S(1)} %get-tuple-element.100, s32[2,4096]{1,0:T(2,128)S(1)} %dynamic-slice_bitcast_fusion.2), kind=kOutput, calls=%fused_computation.6.clone.1 | convolution fusion | flops 73400320 | bytes 475140 | tf_op jit(solution)/shard_map/while/body/eval_jaxpr/skr,krb->ksb/dot_general | solution.py:15
  89.6 1.6 %fusion.31 = f32[16,2,17,256]{3,2,1,0:T(8,128)S(1)} fusion(f32[16,2,17,256]{3,2,1,0:T(8,128)S(1)} %get-tuple-element.93, s32[]{:T(128)} %get-tuple-element.92, bf16[17,2,4096]{2,0,1:T(8,128)(2,1)S(1)} %get-tuple-element.100, s32[2,4096]{1,0:T(2,128)S(1)} %dynamic-slice_bitcast_fusion.2), kind=kOutput, calls=%fused_computation.6.clone.1 | convolution fusion | flops 73400320 | bytes 475140 | tf_op jit(solution)/shard_map/while/body/eval_jaxpr/skr,krb->ksb/dot_general | solution.py:15
  91.3 1.6 %fusion.31 = f32[16,2,17,256]{3,2,1,0:T(8,128)S(1)} fusion(f32[16,2,17,256]{3,2,1,0:T(8,128)S(1)} %get-tuple-element.93, s32[]{:T(128)} %get-tuple-element.92, bf16[17,2,4096]{2,0,1:T(8,128)(2,1)S(1)} %get-tuple-element.100, s32[2,4096]{1,0:T(2,128)S(1)} %dynamic-slice_bitcast_fusion.2), kind=kOutput, calls=%fused_computation.6.clone.1 | convolution fusion | flops 73400320 | bytes 475140 | tf_op jit(solution)/shard_map/while/body/eval_jaxpr/skr,krb->ksb/dot_general | solution.py:15
  93.0 1.6 %fusion.31 = f32[16,2,17,256]{3,2,1,0:T(8,128)S(1)} fusion(f32[16,2,17,256]{3,2,1,0:T(8,128)S(1)} %get-tuple-element.93, s32[]{:T(128)} %get-tuple-element.92, bf16[17,2,4096]{2,0,1:T(8,128)(2,1)S(1)} %get-tuple-element.100, s32[2,4096]{1,0:T(2,128)S(1)} %dynamic-slice_bitcast_fusion.2), kind=kOutput, calls=%fused_computation.6.clone.1 | convolution fusion | flops 73400320 | bytes 475140 | tf_op jit(solution)/shard_map/while/body/eval_jaxpr/skr,krb->ksb/dot_general | solution.py:15
  94.7 1.6 %fusion.31 = f32[16,2,17,256]{3,2,1,0:T(8,128)S(1)} fusion(f32[16,2,17,256]{3,2,1,0:T(8,128)S(1)} %get-tuple-element.93, s32[]{:T(128)} %get-tuple-element.92, bf16[17,2,4096]{2,0,1:T(8,128)(2,1)S(1)} %get-tuple-element.100, s32[2,4096]{1,0:T(2,128)S(1)} %dynamic-slice_bitcast_fusion.2), kind=kOutput, calls=%fused_computation.6.clone.1 | convolution fusion | flops 73400320 | bytes 475140 | tf_op jit(solution)/shard_map/while/body/eval_jaxpr/skr,krb->ksb/dot_general | solution.py:15
  96.3 0.5 fusion.7
  96.9 0.3 slice_reduce_fusion.1
  97.2 0.2 broadcast_subtract_fusion
  97.3 0.3 fusion.9
  97.6 0.4 fusion.13
  98.1 0.4 fusion.23
  98.5 0.2 fusion.22
  98.7 0.6 broadcast_in_dim.34
  99.3 6.8 %all-to-all-start.1 = ((f32[16,1,2]{2,1,0:T(1,128)}), f32[16,1,2]{2,1,0:T(1,128)S(1)}, u32[]{:S(2)}, u32[]{:S(2)}) async-start(f32[16,1,2]{2,1,0:T(1,128)} %broadcast_in_dim.34), calls=%async_computation.1 | async-start | bytes 16384 | tf_op jit(solution)/shard_map/all_to_all | solution.py:78
  106.1 1.1 %copy.80 = f32[16,2,17,256]{3,0,2,1:T(8,128)} copy(f32[16,2,17,256]{3,2,1,0:T(8,128)S(1)} %get-tuple-element.29) | data formatting | bytes 1114112 | tf_op jit(solution)/shard_map/while | solution.py:17
  107.2 5.3 %all-to-all-done.1 = f32[16,1,2]{2,1,0:T(1,128)S(1)} async-done(((f32[16,1,2]{2,1,0:T(1,128)}), f32[16,1,2]{2,1,0:T(1,128)S(1)}, u32[]{:S(2)}, u32[]{:S(2)}) %all-to-all-start.1) | async-done | bytes 160 | tf_op jit(solution)/shard_map/all_to_all | solution.py:78
  112.5 0.5 reduce_max.19
  (34 shorter events, 0.3 us)
Async XLA Ops:
  0.6 3.1 %copy-start.2 = (s32[4096]{0:T(1024)S(1)}, s32[4096]{0:T(1024)}, u32[]{:S(2)}) copy-start(s32[4096]{0:T(1024)} %param.9) | copy-start | bytes 49156
  0.6 3.1 %copy-start.1 = (bf16[16,4096]{1,0:T(8,128)(2,1)S(1)}, bf16[16,4096]{1,0:T(8,128)(2,1)}, u32[]{:S(2)}) copy-start(bf16[16,4096]{1,0:T(8,128)(2,1)} %param.7) | copy-start | bytes 393220
  0.7 3.1 %copy-start = (bf16[16,4096]{1,0:T(8,128)(2,1)S(1)}, bf16[16,4096]{1,0:T(8,128)(2,1)}, u32[]{:S(2)}) copy-start(bf16[16,4096]{1,0:T(8,128)(2,1)} %param.8) | copy-start | bytes 393220
  18.1 50.3 %all-to-all-start = ((bf16[32,32,2,128]{3,0,2,1:T(8,128)(2,1)}), bf16[32,32,2,128]{3,0,2,1:T(8,128)(2,1)S(1)}, u32[]{:S(2)}, u32[]{:S(2)}) async-start(bf16[32,32,2,128]{3,0,2,1:T(8,128)(2,1)} %copy.46), calls=%async_computation | async-start | bytes 1048576 | tf_op jit(solution)/shard_map/all_to_all | solution.py:61
  99.3 13.2 %all-to-all-start.1 = ((f32[16,1,2]{2,1,0:T(1,128)}), f32[16,1,2]{2,1,0:T(1,128)S(1)}, u32[]{:S(2)}, u32[]{:S(2)}) async-start(f32[16,1,2]{2,1,0:T(1,128)} %broadcast_in_dim.34), calls=%async_computation.1 | async-start | bytes 16384 | tf_op jit(solution)/shard_map/all_to_all | solution.py:78

commit v4 on v3

--- a/solution.py
+++ b/solution.py
@@ -1,22 +1,61 @@
 import jax
 import jax.numpy as jnp
 from jax import lax
+from jax.experimental import pallas as pl
+from jax.experimental.pallas import tpu as pltpu
 from jax.sharding import PartitionSpec as P
 
 B = 256
 BLOCK = 256
+CH = 512
 
 
-def feature_histograms(bin_table, statistics):
-    levels = lax.broadcasted_iota(jnp.int32, (1, 1, B), 2)
+def histogram_kernel(bins_ref, stats_ref, hist_ref, best_ref):
+    feats = bins_ref.shape[1]
+    slots = bins_ref.shape[2]
+    stat_count = stats_ref.shape[1]
+    levels = lax.broadcasted_iota(jnp.int32, (B, CH), 0)
+    c = lax.broadcasted_iota(jnp.int32, (B, B), 0)
+    b = lax.broadcasted_iota(jnp.int32, (B, B), 1)
+    upper = (c <= b).astype(jnp.bfloat16)
+    best = jnp.full((1, B), -jnp.inf, jnp.float32)
+    for f in range(feats):
+        acc = jnp.zeros((stat_count, B), jnp.float32)
+        for k in range(slots // CH):
+            row = bins_ref[0, f:f + 1, k * CH:(k + 1) * CH]
+            indicator = (levels == row).astype(jnp.bfloat16)
+            acc = acc + lax.dot_general(
+                stats_ref[0, :, k * CH:(k + 1) * CH], indicator, (((1,), (1,)), ((), ())),
+                preferred_element_type=jnp.float32)
+        hist_ref[0, f] = acc
+    lane = lax.broadcasted_iota(jnp.int32, (stat_count, B), 1)
+    for f in range(feats):
+        left = hist_ref[0, f]
+        shift = 1
+        while shift < B:
+            moved = pltpu.roll(left, shift, 1)
+            left = left + jnp.where(lane >= shift, moved, 0.0)
+            shift *= 2
+        total = left[:, B - 1:B]
+        right = total - left
+        left_part = jnp.sum(left[1:] * left[1:], axis=0, keepdims=True) / (left[0:1] + 1.0)
+        right_part = jnp.sum(right[1:] * right[1:], axis=0, keepdims=True) / (right[0:1] + 1.0)
+        total_part = jnp.sum(total[1:] * total[1:], axis=0, keepdims=True) / (total[0:1] + 1.0)
+        best = jnp.maximum(best, left_part + right_part - total_part)
+    best_ref[0] = jnp.broadcast_to(jnp.max(best, axis=1, keepdims=True), (8, 128))
 
-    def one_feature(bin_row):
-        indicator = (bin_row[:, :, None] == levels).astype(jnp.bfloat16)
-        return jnp.einsum("skr,krb->ksb", statistics, indicator, preferred_element_type=jnp.float32)
-
-    stacked = lax.map(one_feature, bin_table)
-    return jnp.transpose(stacked, (1, 0, 2, 3))
-
+def hist_and_best(bins, stats):
+    nodes, feats, slots = bins.shape
+    st = stats.shape[1]
+    hist, best = pl.pallas_call(
+        histogram_kernel, grid=(nodes,),
+        in_specs=[pl.BlockSpec((1, feats, slots), lambda n: (n, 0, 0)),
+                  pl.BlockSpec((1, st, slots), lambda n: (n, 0, 0))],
+        out_specs=[pl.BlockSpec((1, feats, st, B), lambda n: (n, 0, 0, 0)),
+                   pl.BlockSpec((1, 8, 128), lambda n: (n, 0, 0))],
+        out_shape=[jax.ShapeDtypeStruct((nodes, feats, st, B), jnp.float32),
+                   jax.ShapeDtypeStruct((nodes, 8, 128), jnp.float32)])(bins, stats)
+    return hist, best[:, 0, 0]
 
 def running_rank(owned):
     rows, nodes = owned.shape
@@ -60,20 +99,10 @@
     outgoing = outgoing.reshape(payload_width, node_devices, node_local, capacity)
     arrived = lax.all_to_all(outgoing, "node", split_axis=1, concat_axis=3, tiled=True)[:, 0]
     bin_table = jnp.floor(arrived[:feat_count].astype(jnp.float32) * B).astype(jnp.int32)
-    ones = jnp.ones((1,) + arrived.shape[1:], jnp.bfloat16)
-    statistics = jnp.concatenate([ones, arrived[feat_count:]], axis=0)
-    histogram = feature_histograms(bin_table, statistics)
-    c = lax.broadcasted_iota(jnp.int32, (B, B), 0)
-    b = lax.broadcasted_iota(jnp.int32, (B, B), 1)
-    upper = (c <= b).astype(jnp.float32)
-    left = jnp.einsum("nfsc,cb->nfsb", histogram, upper, precision=lax.Precision.HIGHEST)
-    total = left[:, :, :, -1:]
-    right = total - left
-    left_part = jnp.sum(left[:, :, 1:] * left[:, :, 1:], axis=2) / (left[:, :, 0] + 1.0)
-    right_part = jnp.sum(right[:, :, 1:] * right[:, :, 1:], axis=2) / (right[:, :, 0] + 1.0)
-    total_part = jnp.sum(total[:, :, 1:] * total[:, :, 1:], axis=2) / (total[:, :, 0] + 1.0)
-    gain = left_part + right_part - total_part
-    best_local = jnp.max(gain, axis=(1, 2))
+    bin_table = jnp.transpose(bin_table, (1, 0, 2))
+    ones = jnp.ones((node_local, 1, arrived.shape[2]), jnp.bfloat16)
+    statistics = jnp.concatenate([ones, jnp.transpose(arrived[feat_count:], (1, 0, 2))], axis=1)
+    histogram, best_local = hist_and_best(bin_table, statistics)
     spread = jnp.broadcast_to(best_local[None, :], (feat_devices, node_local))
     gathered = lax.all_to_all(spread, "feat", split_axis=0, concat_axis=0, tiled=True)
     best_gain = jnp.max(gathered, axis=0)

time: 114 us -> 109 us (0.956)
  blocking collectives: 0 us -> 50.1 us
  waiting for transfers between devices: 38.8 us -> 4.3 us
  matrix products: 27.3 us -> 0.49 us
  Pallas kernels: 0 us -> 23 us
  starting transfers between devices: 23.5 us -> 6.76 us
  local copies, waits for them, and re-layouts: 17.8 us -> 19.8 us
    all_to_all x0 -> x1, blocking collectives: none -> 50.1 us  [on_device(): lax.all_to_all(outgoing, 'node', split_axis=1, concat_axis=3, tiled=True)]
    all_to_all x1 -> x0, waiting for transfers between devices: 33.5 us -> none  [on_device(): lax.all_to_all(outgoing, 'node', split_axis=1, concat_axis=3, tiled=True)]
    dot_general x17 -> x0, matrix products: 26.8 us -> none  [the longest x16 26.3 us: one_feature(): jnp.einsum('skr,krb->ksb', statistics, indicator, preferred_element_type=...]
    pallas_call x0 -> x1, Pallas kernels: none -> 23 us  [hist_and_best(): pl.pallas_call(histogram_kernel, grid=(nodes,), in_specs=[pl.BlockSpec((1...]
    all_to_all x1 -> x0, starting transfers between devices: 16.7 us -> none  [on_device(): lax.all_to_all(outgoing, 'node', split_axis=1, concat_axis=3, tiled=True)]
    unnamed x9 -> x4, local copies, waits for them, and re-layouts: 0.61 us -> 2.12 us
    convert_element_type x0 -> x2, local copies, waits for them, and re-layouts: none -> 1.2 us  [on_device(): jnp.floor(arrived[:feat_count].astype(jnp.float32) * B).astype(jnp.int32)]
  transfers between devices with their start and end apart: 2 -> 1, of which waited for: 2 -> 1; matrix products, arithmetic and copies ran while one was open for 1% -> 2% of each run, Pallas kernels for 0% -> 0%
where the time goes in v4:
time: 109 us
  blocking collectives  50.1 us (46%)
  Pallas kernels  23 us (21%)
  local copies, waits for them, and re-layouts  19.8 us (18%)
  starting transfers between devices  6.76 us (6%)
  waiting for transfers between devices  4.3 us (4%)
  other arithmetic  3.73 us (3%)
    all_to_all x1, blocking collectives, on_device(): lax.all_to_all(outgoing, 'node', split_axis=1, concat_axis=3, tiled=True)  50.1 us
    pallas_call x1, Pallas kernels, hist_and_best(): pl.pallas_call(histogram_kernel, grid=(nodes,), in_specs=[pl.BlockSpec((1...  23 us
    scatter x1, local copies, waits for them, and re-layouts, on_device(): outgoing = empty.at[:, position].set(payload, mode='drop')  12 us
    all_to_all x1, starting transfers between devices, on_device(): lax.all_to_all(spread, 'feat', split_axis=0, concat_axis=0, tiled=True)  6.76 us
    all_to_all x1, waiting for transfers between devices, on_device(): lax.all_to_all(spread, 'feat', split_axis=0, concat_axis=0, tiled=True)  4.3 us
  transfers between devices with their start and end apart: 1, of which 1 were waited for; matrix products, arithmetic and copies ran while one was open for 2% of the time, Pallas kernels for 0%

profile of v4, /device:TPU:1, one launch (start us, length us, event | category | flops | bytes accessed | tf_op | source)
XLA Modules:
  0.0 108.9 jit_solution(10915841591693499141)
XLA Ops:
  0.6 0.7 broadcast_compare_fusion
  1.4 1.0 select_reduce_fusion
  2.4 1.0 maximum_bitcast_fusion
  3.3 0.0 copy-start
  3.4 0.5 copy.23
  3.8 0.4 convolution_bitcast_fusion
  4.2 0.4 slice_reduce_fusion
  4.6 0.1 fusion.5
  4.7 0.4 multiply_reduce_fusion
  5.2 0.0 copy-done
  5.2 0.3 concatenate.12
  5.5 12.0 %scatter_fusion = bf16[32,8192]{0,1:T(8,128)(2,1)S(1)} fusion(bf16[32,8192]{0,1:T(8,128)(2,1)S(1)} %concatenate.12, s32[4096]{0:T(1024)S(1)} %compare_select_fusion, bf16[4096,32]{1,0:T(8,128)(2,1)S(1)} %copy.23), kind=kCustom, calls=%fused_computation | custom fusion | bytes 802816 | tf_op jit(solution)/shard_map/scatter | solution.py:98
  17.5 0.9 copy.24
  18.3 50.1 %all_to_all.21 = bf16[32,32,2,128]{3,0,2,1:T(8,128)(2,1)S(1)} all-to-all(bf16[32,32,2,128]{3,0,2,1:T(8,128)(2,1)S(1)} %copy.24), channel_id=1, replica_groups=mesh['node'=32,'feat'=16] {'node'}, dimensions={1} | all-to-all | bytes 1048576 | tf_op jit(solution)/shard_map/all_to_all | solution.py:100
  68.4 0.1 floor_convert_fusion
  68.5 0.3 copy.25
  68.8 0.9 convert_element_type.33
  69.7 0.1 copy.26
  69.8 0.1 slice.19
  70.0 0.8 concatenate.14.stats_ref
  70.8 23.0 %shard_map.68 = (f32[2,16,17,256]{3,2,1,0:T(8,128)}, f32[2,8,128]{2,1,0:T(8,128)}) custom-call(s32[2,16,4096]{2,1,0:T(8,128)} %bitcast.28, bf16[2,17,4096]{2,1,0:T(8,128)(2,1)} %concatenate.14.stats_ref), custom_call_target="tpu_custom_call" | custom-call | tf_op jit(solution)/shard_map/pallas_call | solution.py:50
  93.7 0.8 slice_reduce_fusion.1
  94.5 0.6 broadcast_in_dim.27
  95.1 6.8 %all-to-all-start.1 = ((f32[16,1,2]{2,1,0:T(1,128)}), f32[16,1,2]{2,1,0:T(1,128)S(1)}, u32[]{:S(2)}, u32[]{:S(2)}) async-start(f32[16,1,2]{2,1,0:T(1,128)} %broadcast_in_dim.27), calls=%async_computation.1 | async-start | bytes 16384 | tf_op jit(solution)/shard_map/all_to_all | solution.py:107
  101.9 2.1 %copy.28 = f32[2,16,17,256]{3,1,2,0:T(8,128)} copy(f32[2,16,17,256]{3,2,1,0:T(8,128)} %get-tuple-element.14) | data formatting | bytes 1114112
  104.0 4.3 %all-to-all-done.1 = f32[16,1,2]{2,1,0:T(1,128)S(1)} async-done(((f32[16,1,2]{2,1,0:T(1,128)}), f32[16,1,2]{2,1,0:T(1,128)S(1)}, u32[]{:S(2)}, u32[]{:S(2)}) %all-to-all-start.1) | async-done | bytes 160 | tf_op jit(solution)/shard_map/all_to_all | solution.py:107
  108.3 0.5 reduce_max.9
  (8 shorter events, 0.1 us)
Async XLA Ops:
  3.3 1.8 %copy-start = (s32[4096]{0:T(1024)S(1)}, s32[4096]{0:T(1024)}, u32[]{:S(2)}) copy-start(s32[4096]{0:T(1024)} %param.7) | copy-start | bytes 49156
  95.1 13.2 %all-to-all-start.1 = ((f32[16,1,2]{2,1,0:T(1,128)}), f32[16,1,2]{2,1,0:T(1,128)S(1)}, u32[]{:S(2)}, u32[]{:S(2)}) async-start(f32[16,1,2]{2,1,0:T(1,128)} %broadcast_in_dim.27), calls=%async_computation.1 | async-start | bytes 16384 | tf_op jit(solution)/shard_map/all_to_all | solution.py:107

commit v5 on v4

--- a/solution.py
+++ b/solution.py
@@ -10,24 +10,26 @@
 CH = 512
 
 
-def histogram_kernel(bins_ref, stats_ref, hist_ref, best_ref):
+def histogram_kernel(flags_ref, bins_ref, stats_ref, hist_ref, best_ref):
     feats = bins_ref.shape[1]
     slots = bins_ref.shape[2]
     stat_count = stats_ref.shape[1]
+    chunks = slots // CH
+    node = pl.program_id(0)
     levels = lax.broadcasted_iota(jnp.int32, (B, CH), 0)
-    c = lax.broadcasted_iota(jnp.int32, (B, B), 0)
-    b = lax.broadcasted_iota(jnp.int32, (B, B), 1)
-    upper = (c <= b).astype(jnp.bfloat16)
     best = jnp.full((1, B), -jnp.inf, jnp.float32)
-    for f in range(feats):
-        acc = jnp.zeros((stat_count, B), jnp.float32)
-        for k in range(slots // CH):
-            row = bins_ref[0, f:f + 1, k * CH:(k + 1) * CH]
-            indicator = (levels == row).astype(jnp.bfloat16)
-            acc = acc + lax.dot_general(
-                stats_ref[0, :, k * CH:(k + 1) * CH], indicator, (((1,), (1,)), ((), ())),
-                preferred_element_type=jnp.float32)
-        hist_ref[0, f] = acc
+    hist_ref[...] = jnp.zeros(hist_ref.shape, hist_ref.dtype)
+    for k in range(chunks):
+
+        @pl.when(flags_ref[node * chunks + k] > 0)
+        def _():
+            for f in range(feats):
+                row = bins_ref[0, f:f + 1, k * CH:(k + 1) * CH]
+                indicator = (levels == row).astype(jnp.bfloat16)
+                hist_ref[0, f] += lax.dot_general(
+                    stats_ref[0, :, k * CH:(k + 1) * CH], indicator, (((1,), (1,)), ((), ())),
+                    preferred_element_type=jnp.float32)
+
     lane = lax.broadcasted_iota(jnp.int32, (stat_count, B), 1)
     for f in range(feats):
         left = hist_ref[0, f]
@@ -47,15 +49,22 @@
 def hist_and_best(bins, stats):
     nodes, feats, slots = bins.shape
     st = stats.shape[1]
+    chunks = slots // CH
+    filled = jnp.any(bins[:, 0].reshape(nodes, chunks, CH) < B, axis=2)
+    flags = filled.astype(jnp.int32).reshape(nodes * chunks)
     hist, best = pl.pallas_call(
-        histogram_kernel, grid=(nodes,),
-        in_specs=[pl.BlockSpec((1, feats, slots), lambda n: (n, 0, 0)),
-                  pl.BlockSpec((1, st, slots), lambda n: (n, 0, 0))],
-        out_specs=[pl.BlockSpec((1, feats, st, B), lambda n: (n, 0, 0, 0)),
-                   pl.BlockSpec((1, 8, 128), lambda n: (n, 0, 0))],
+        histogram_kernel,
+        grid_spec=pltpu.PrefetchScalarGridSpec(
+            num_scalar_prefetch=1,
+            grid=(nodes,),
+            in_specs=[pl.BlockSpec((1, feats, slots), lambda n, fl: (n, 0, 0)),
+                      pl.BlockSpec((1, st, slots), lambda n, fl: (n, 0, 0))],
+            out_specs=[pl.BlockSpec((1, feats, st, B), lambda n, fl: (n, 0, 0, 0)),
+                       pl.BlockSpec((1, 8, 128), lambda n, fl: (n, 0, 0))]),
         out_shape=[jax.ShapeDtypeStruct((nodes, feats, st, B), jnp.float32),
-                   jax.ShapeDtypeStruct((nodes, 8, 128), jnp.float32)])(bins, stats)
+                   jax.ShapeDtypeStruct((nodes, 8, 128), jnp.float32)])(flags, bins, stats)
     return hist, best[:, 0, 0]
+
 
 def running_rank(owned):
     rows, nodes = owned.shape
@@ -98,6 +107,8 @@
     outgoing = empty.at[:, position].set(payload, mode="drop")
     outgoing = outgoing.reshape(payload_width, node_devices, node_local, capacity)
     arrived = lax.all_to_all(outgoing, "node", split_axis=1, concat_axis=3, tiled=True)[:, 0]
+    arrived = arrived.reshape(payload_width, node_local, node_devices, capacity)
+    arrived = jnp.transpose(arrived, (0, 1, 3, 2)).reshape(payload_width, node_local, node_devices * capacity)
     bin_table = jnp.floor(arrived[:feat_count].astype(jnp.float32) * B).astype(jnp.int32)
     bin_table = jnp.transpose(bin_table, (1, 0, 2))
     ones = jnp.ones((node_local, 1, arrived.shape[2]), jnp.bfloat16)

time: 109 us -> 105 us (0.963)
  the two profiles are of different devices: /device:TPU:1 before, /device:TPU:2 now
where the time goes in v5:
time: 105 us
  blocking collectives  49 us (47%)
  local copies, waits for them, and re-layouts  22.2 us (21%)
  Pallas kernels  16.8 us (16%)
  starting transfers between devices  7.48 us (7%)
  waiting for transfers between devices  4.09 us (4%)
  other arithmetic  3.99 us (4%)
    all_to_all x1, blocking collectives, on_device(): lax.all_to_all(outgoing, 'node', split_axis=1, concat_axis=3, tiled=True)  49 us
    pallas_call x1, Pallas kernels, hist_and_best(): pl.pallas_call(histogram_kernel, grid_spec=pltpu.PrefetchScalarGridSpec(n...  16.8 us
    scatter x1, local copies, waits for them, and re-layouts, on_device(): outgoing = empty.at[:, position].set(payload, mode='drop')  12 us
    all_to_all x1, starting transfers between devices, on_device(): lax.all_to_all(spread, 'feat', split_axis=0, concat_axis=0, tiled=True)  7.48 us
    all_to_all x1, waiting for transfers between devices, on_device(): lax.all_to_all(spread, 'feat', split_axis=0, concat_axis=0, tiled=True)  4.09 us
    unnamed x6, local copies, waits for them, and re-layouts  2.13 us
  transfers between devices with their start and end apart: 1, of which 1 were waited for; matrix products, arithmetic and copies ran while one was open for 2% of the time, Pallas kernels for 0%

profile of v5, /device:TPU:2, one launch (start us, length us, event | category | flops | bytes accessed | tf_op | source)
XLA Modules:
  0.0 104.9 jit_solution(1525102475249041049)
XLA Ops:
  0.6 0.7 broadcast_compare_fusion
  1.4 1.0 select_reduce_fusion
  2.4 1.0 maximum_bitcast_fusion
  3.3 0.0 copy-start.1
  3.4 0.5 copy.23
  3.8 0.4 convolution_bitcast_fusion
  4.2 0.4 slice_reduce_fusion
  4.6 0.1 fusion.5
  4.7 0.4 multiply_reduce_fusion
  5.2 0.0 copy-done.1
  5.2 0.3 concatenate.12
  5.5 12.0 %scatter_fusion = bf16[32,8192]{0,1:T(8,128)(2,1)S(1)} fusion(bf16[32,8192]{0,1:T(8,128)(2,1)S(1)} %concatenate.12, s32[4096]{0:T(1024)S(1)} %compare_select_fusion, bf16[4096,32]{1,0:T(8,128)(2,1)S(1)} %copy.23), kind=kCustom, calls=%fused_computation | custom fusion | bytes 802816 | tf_op jit(solution)/shard_map/scatter | solution.py:107
  17.5 0.9 copy.24
  18.3 49.0 %all_to_all.21 = bf16[32,32,2,128]{3,0,2,1:T(8,128)(2,1)S(1)} all-to-all(bf16[32,32,2,128]{3,0,2,1:T(8,128)(2,1)S(1)} %copy.24), channel_id=1, replica_groups=mesh['node'=32,'feat'=16] {'node'}, dimensions={1} | all-to-all | bytes 1048576 | tf_op jit(solution)/shard_map/all_to_all | solution.py:109
  67.4 0.1 floor_convert_fusion
  67.5 0.5 copy.26
  68.0 1.1 %slice.23 = bf16[16,2,4096]{2,0,1:T(8,128)(2,1)S(1)} reshape(bf16[16,2,128,32]{3,2,0,1:T(8,128)(2,1)S(1)} %copy.26) | data formatting | bytes 524288 | tf_op jit(solution)/shard_map/slice | solution.py:115
  69.2 0.8 concatenate.14.stats_ref
  70.0 0.6 copy.25
  70.6 1.0 convert_element_type.40
  71.6 0.0 copy-start
  71.6 0.1 compare_reduce_fusion
  71.7 0.1 bitcast_reduce_fusion
  71.9 0.6 reshape.53.flags_ref
  72.5 0.0 copy-done
  72.5 16.8 %shard_map.68 = (f32[2,16,17,256]{3,2,1,0:T(8,128)}, f32[2,8,128]{2,1,0:T(8,128)}) custom-call(s32[16]{0:T(128)} %reshape.53.flags_ref, s32[2,16,4096]{2,1,0:T(8,128)} %bitcast.36, bf16[2,17,4096]{2,1,0:T(8,128)(2,1)} %concatenate.14.stats_ref), custom_call_target="tpu_custom_call" | custom-call | tf_op jit(solution)/shard_map/pallas_call | solution.py:55
  89.2 0.8 slice_reduce_fusion.1
  90.0 0.6 broadcast_in_dim.27
  90.6 7.5 %all-to-all-start.1 = ((f32[16,1,2]{2,1,0:T(1,128)}), f32[16,1,2]{2,1,0:T(1,128)S(1)}, u32[]{:S(2)}, u32[]{:S(2)}) async-start(f32[16,1,2]{2,1,0:T(1,128)} %broadcast_in_dim.27), calls=%async_computation.1 | async-start | bytes 16384 | tf_op jit(solution)/shard_map/all_to_all | solution.py:118
  98.1 2.1 %copy.28 = f32[2,16,17,256]{3,1,2,0:T(8,128)} copy(f32[2,16,17,256]{3,2,1,0:T(8,128)} %get-tuple-element.14) | data formatting | bytes 1114112
  100.2 4.1 %all-to-all-done.1 = f32[16,1,2]{2,1,0:T(1,128)S(1)} async-done(((f32[16,1,2]{2,1,0:T(1,128)}), f32[16,1,2]{2,1,0:T(1,128)S(1)}, u32[]{:S(2)}, u32[]{:S(2)}) %all-to-all-start.1) | async-done | bytes 160 | tf_op jit(solution)/shard_map/all_to_all | solution.py:118
  104.3 0.5 reduce_max.9
  (9 shorter events, 0.1 us)
Async XLA Ops:
  3.3 1.8 %copy-start.1 = (s32[4096]{0:T(1024)S(1)}, s32[4096]{0:T(1024)}, u32[]{:S(2)}) copy-start(s32[4096]{0:T(1024)} %param.7) | copy-start | bytes 49156
  71.6 0.9 copy-start
  90.6 13.7 %all-to-all-start.1 = ((f32[16,1,2]{2,1,0:T(1,128)}), f32[16,1,2]{2,1,0:T(1,128)S(1)}, u32[]{:S(2)}, u32[]{:S(2)}) async-start(f32[16,1,2]{2,1,0:T(1,128)} %broadcast_in_dim.27), calls=%async_computation.1 | async-start | bytes 16384 | tf_op jit(solution)/shard_map/all_to_all | solution.py:118

commit v6 on v5

--- a/solution.py
+++ b/solution.py
@@ -104,11 +104,11 @@
     empty = jnp.concatenate(
         [jnp.ones((feat_count, slots), jnp.bfloat16), jnp.zeros((payload_width - feat_count, slots), jnp.bfloat16)]
     )
-    outgoing = empty.at[:, position].set(payload, mode="drop")
-    outgoing = outgoing.reshape(payload_width, node_devices, node_local, capacity)
-    arrived = lax.all_to_all(outgoing, "node", split_axis=1, concat_axis=3, tiled=True)[:, 0]
-    arrived = arrived.reshape(payload_width, node_local, node_devices, capacity)
-    arrived = jnp.transpose(arrived, (0, 1, 3, 2)).reshape(payload_width, node_local, node_devices * capacity)
+    outgoing = empty.T.at[position].set(payload.T, mode="drop")
+    outgoing = outgoing.reshape(node_devices, node_local * capacity, payload_width)
+    arrived = lax.all_to_all(outgoing, "node", split_axis=0, concat_axis=0, tiled=True)
+    arrived = arrived.reshape(node_devices, node_local, capacity, payload_width)
+    arrived = jnp.transpose(arrived, (3, 1, 2, 0)).reshape(payload_width, node_local, capacity * node_devices)
     bin_table = jnp.floor(arrived[:feat_count].astype(jnp.float32) * B).astype(jnp.int32)
     bin_table = jnp.transpose(bin_table, (1, 0, 2))
     ones = jnp.ones((node_local, 1, arrived.shape[2]), jnp.bfloat16)

time: 105 us -> 109 us (1.038)
  the two profiles are of different devices: /device:TPU:2 before, /device:TPU:1 now
where the time goes in v6:
time: 109 us
  blocking collectives  50.1 us (46%)
  local copies, waits for them, and re-layouts  22.8 us (21%)
  Pallas kernels  19.4 us (18%)
  starting transfers between devices  6.76 us (6%)
  waiting for transfers between devices  4.3 us (4%)
  other arithmetic  3.99 us (4%)
    all_to_all x1, blocking collectives, on_device(): lax.all_to_all(outgoing, 'node', split_axis=0, concat_axis=0, tiled=True)  50.1 us
    pallas_call x1, Pallas kernels, hist_and_best(): pl.pallas_call(histogram_kernel, grid_spec=pltpu.PrefetchScalarGridSpec(n...  19.4 us
    scatter x1, local copies, waits for them, and re-layouts, on_device(): outgoing = empty.T.at[position].set(payload.T, mode='drop')  12 us
    all_to_all x1, starting transfers between devices, on_device(): lax.all_to_all(spread, 'feat', split_axis=0, concat_axis=0, tiled=True)  6.76 us
    all_to_all x1, waiting for transfers between devices, on_device(): lax.all_to_all(spread, 'feat', split_axis=0, concat_axis=0, tiled=True)  4.3 us
  transfers between devices with their start and end apart: 1, of which 1 were waited for; matrix products, arithmetic and copies ran while one was open for 2% of the time, Pallas kernels for 0%

profile of v6, /device:TPU:1, one launch (start us, length us, event | category | flops | bytes accessed | tf_op | source)
XLA Modules:
  0.0 108.6 jit_solution(12923870457997911564)
XLA Ops:
  0.6 0.7 broadcast_compare_fusion
  1.4 1.0 select_reduce_fusion
  2.4 1.0 maximum_bitcast_fusion
  3.3 0.0 copy-start.1
  3.4 0.5 copy.25
  3.8 0.4 convolution_bitcast_fusion
  4.2 0.4 slice_reduce_fusion
  4.6 0.1 fusion.5
  4.7 0.4 multiply_reduce_fusion
  5.2 0.0 copy-done.1
  5.2 0.3 transpose.25
  5.5 12.0 %scatter_fusion = bf16[8192,32]{1,0:T(8,128)(2,1)S(1)} fusion(bf16[8192,32]{1,0:T(8,128)(2,1)S(1)} %transpose.25, s32[4096]{0:T(1024)S(1)} %compare_select_fusion, bf16[4096,32]{1,0:T(8,128)(2,1)S(1)} %copy.25), kind=kCustom, calls=%fused_computation | custom fusion | bytes 802816 | tf_op jit(solution)/shard_map/scatter | solution.py:107
  17.5 0.8 copy.26
  18.3 50.1 %all_to_all.11 = bf16[32,256,32]{1,2,0:T(8,128)(2,1)S(1)} all-to-all(bf16[32,256,32]{1,2,0:T(8,128)(2,1)S(1)} %copy.26), channel_id=1, replica_groups=mesh['node'=32,'feat'=16] {'node'}, dimensions={0} | all-to-all | bytes 1048576 | tf_op jit(solution)/shard_map/all_to_all | solution.py:109
  68.3 0.1 reshape.55
  68.5 0.6 copy.37
  69.1 0.1 floor_convert_fusion
  69.2 0.5 copy.29
  69.7 1.1 %slice.23 = bf16[16,2,4096]{2,0,1:T(8,128)(2,1)S(1)} reshape(bf16[16,2,128,32]{3,2,0,1:T(8,128)(2,1)S(1)} %copy.29) | data formatting | bytes 524288 | tf_op jit(solution)/shard_map/slice | solution.py:115
  70.8 0.8 concatenate.11.stats_ref
  71.6 0.6 copy.28
  72.3 1.0 convert_element_type.40
  73.2 0.0 copy-start
  73.2 0.1 compare_reduce_fusion
  73.3 0.1 bitcast_reduce_fusion
  73.5 0.6 reshape.56.flags_ref
  74.1 0.0 copy-done
  74.1 19.4 %shard_map.68 = (f32[2,16,17,256]{3,2,1,0:T(8,128)}, f32[2,8,128]{2,1,0:T(8,128)}) custom-call(s32[16]{0:T(128)} %reshape.56.flags_ref, s32[2,16,4096]{2,1,0:T(8,128)} %bitcast.34, bf16[2,17,4096]{2,1,0:T(8,128)(2,1)} %concatenate.11.stats_ref), custom_call_target="tpu_custom_call" | custom-call | tf_op jit(solution)/shard_map/pallas_call | solution.py:55
  93.5 0.8 slice_reduce_fusion.1
  94.3 0.6 broadcast_in_dim.27
  94.9 6.8 %all-to-all-start.1 = ((f32[16,1,2]{2,1,0:T(1,128)}), f32[16,1,2]{2,1,0:T(1,128)S(1)}, u32[]{:S(2)}, u32[]{:S(2)}) async-start(f32[16,1,2]{2,1,0:T(1,128)} %broadcast_in_dim.27), calls=%async_computation.1 | async-start | bytes 16384 | tf_op jit(solution)/shard_map/all_to_all | solution.py:118
  101.7 2.1 %copy.31 = f32[2,16,17,256]{3,1,2,0:T(8,128)} copy(f32[2,16,17,256]{3,2,1,0:T(8,128)} %get-tuple-element.14) | data formatting | bytes 1114112
  103.8 4.3 %all-to-all-done.1 = f32[16,1,2]{2,1,0:T(1,128)S(1)} async-done(((f32[16,1,2]{2,1,0:T(1,128)}), f32[16,1,2]{2,1,0:T(1,128)S(1)}, u32[]{:S(2)}, u32[]{:S(2)}) %all-to-all-start.1) | async-done | bytes 160 | tf_op jit(solution)/shard_map/all_to_all | solution.py:118
  108.1 0.5 reduce_max.9
  (9 shorter events, 0.1 us)
Async XLA Ops:
  3.3 1.8 %copy-start.1 = (s32[4096]{0:T(1024)S(1)}, s32[4096]{0:T(1024)}, u32[]{:S(2)}) copy-start(s32[4096]{0:T(1024)} %param.7) | copy-start | bytes 49156
  73.2 0.9 copy-start
  94.9 13.2 %all-to-all-start.1 = ((f32[16,1,2]{2,1,0:T(1,128)}), f32[16,1,2]{2,1,0:T(1,128)S(1)}, u32[]{:S(2)}, u32[]{:S(2)}) async-start(f32[16,1,2]{2,1,0:T(1,128)} %broadcast_in_dim.27), calls=%async_computation.1 | async-start | bytes 16384 | tf_op jit(solution)/shard_map/all_to_all | solution.py:118

commit v7 on v6

--- a/solution.py
+++ b/solution.py
@@ -10,25 +10,26 @@
 CH = 512
 
 
-def histogram_kernel(flags_ref, bins_ref, stats_ref, hist_ref, best_ref):
-    feats = bins_ref.shape[1]
-    slots = bins_ref.shape[2]
-    stat_count = stats_ref.shape[1]
+def histogram_kernel(flags_ref, rows_ref, hist_ref, best_ref):
+    feats = hist_ref.shape[1]
+    stat_count = hist_ref.shape[2]
+    slots = rows_ref.shape[2]
     chunks = slots // CH
     node = pl.program_id(0)
-    levels = lax.broadcasted_iota(jnp.int32, (B, CH), 0)
+    levels = lax.broadcasted_iota(jnp.int32, (B, CH), 0).astype(jnp.float32)
     best = jnp.full((1, B), -jnp.inf, jnp.float32)
     hist_ref[...] = jnp.zeros(hist_ref.shape, hist_ref.dtype)
     for k in range(chunks):
 
         @pl.when(flags_ref[node * chunks + k] > 0)
         def _():
+            stats = rows_ref[0, feats:feats + stat_count, k * CH:(k + 1) * CH]
             for f in range(feats):
-                row = bins_ref[0, f:f + 1, k * CH:(k + 1) * CH]
-                indicator = (levels == row).astype(jnp.bfloat16)
+                row = rows_ref[0, f:f + 1, k * CH:(k + 1) * CH]
+                bins = jnp.floor(row.astype(jnp.float32) * B)
+                indicator = (levels == bins).astype(jnp.bfloat16)
                 hist_ref[0, f] += lax.dot_general(
-                    stats_ref[0, :, k * CH:(k + 1) * CH], indicator, (((1,), (1,)), ((), ())),
-                    preferred_element_type=jnp.float32)
+                    stats, indicator, (((1,), (1,)), ((), ())), preferred_element_type=jnp.float32)
 
     lane = lax.broadcasted_iota(jnp.int32, (stat_count, B), 1)
     for f in range(feats):
@@ -46,23 +47,22 @@
         best = jnp.maximum(best, left_part + right_part - total_part)
     best_ref[0] = jnp.broadcast_to(jnp.max(best, axis=1, keepdims=True), (8, 128))
 
-def hist_and_best(bins, stats):
-    nodes, feats, slots = bins.shape
-    st = stats.shape[1]
+def hist_and_best(rows, feats):
+    nodes, width, slots = rows.shape
+    st = width - feats
     chunks = slots // CH
-    filled = jnp.any(bins[:, 0].reshape(nodes, chunks, CH) < B, axis=2)
+    filled = jnp.any(rows[:, 0].reshape(nodes, chunks, CH) < 1.0, axis=2)
     flags = filled.astype(jnp.int32).reshape(nodes * chunks)
     hist, best = pl.pallas_call(
         histogram_kernel,
         grid_spec=pltpu.PrefetchScalarGridSpec(
             num_scalar_prefetch=1,
             grid=(nodes,),
-            in_specs=[pl.BlockSpec((1, feats, slots), lambda n, fl: (n, 0, 0)),
-                      pl.BlockSpec((1, st, slots), lambda n, fl: (n, 0, 0))],
+            in_specs=[pl.BlockSpec((1, width, slots), lambda n, fl: (n, 0, 0))],
             out_specs=[pl.BlockSpec((1, feats, st, B), lambda n, fl: (n, 0, 0, 0)),
                        pl.BlockSpec((1, 8, 128), lambda n, fl: (n, 0, 0))]),
         out_shape=[jax.ShapeDtypeStruct((nodes, feats, st, B), jnp.float32),
-                   jax.ShapeDtypeStruct((nodes, 8, 128), jnp.float32)])(flags, bins, stats)
+                   jax.ShapeDtypeStruct((nodes, 8, 128), jnp.float32)])(flags, rows)
     return hist, best[:, 0, 0]
 
 
@@ -99,7 +99,8 @@
     rank = running_rank(owned)
     slots = node_total * capacity
     position = jnp.where(kept, target * capacity + rank, slots)
-    payload = jnp.concatenate([covariates, pseudo], axis=0)
+    weight_row = jnp.ones((1, row_count), jnp.bfloat16)
+    payload = jnp.concatenate([covariates, weight_row, pseudo], axis=0)
     payload_width = payload.shape[0]
     empty = jnp.concatenate(
         [jnp.ones((feat_count, slots), jnp.bfloat16), jnp.zeros((payload_width - feat_count, slots), jnp.bfloat16)]
@@ -108,12 +109,8 @@
     outgoing = outgoing.reshape(node_devices, node_local * capacity, payload_width)
     arrived = lax.all_to_all(outgoing, "node", split_axis=0, concat_axis=0, tiled=True)
     arrived = arrived.reshape(node_devices, node_local, capacity, payload_width)
-    arrived = jnp.transpose(arrived, (3, 1, 2, 0)).reshape(payload_width, node_local, capacity * node_devices)
-    bin_table = jnp.floor(arrived[:feat_count].astype(jnp.float32) * B).astype(jnp.int32)
-    bin_table = jnp.transpose(bin_table, (1, 0, 2))
-    ones = jnp.ones((node_local, 1, arrived.shape[2]), jnp.bfloat16)
-    statistics = jnp.concatenate([ones, jnp.transpose(arrived[feat_count:], (1, 0, 2))], axis=1)
-    histogram, best_local = hist_and_best(bin_table, statistics)
+    rows = jnp.transpose(arrived, (1, 3, 2, 0)).reshape(node_local, payload_width, capacity * node_devices)
+    histogram, best_local = hist_and_best(rows, feat_count)
     spread = jnp.broadcast_to(best_local[None, :], (feat_devices, node_local))
     gathered = lax.all_to_all(spread, "feat", split_axis=0, concat_axis=0, tiled=True)
     best_gain = jnp.max(gathered, axis=0)

time: 109 us -> 113 us (1.037)
  the two profiles are of different devices: /device:TPU:1 before, /device:TPU:2 now
where the time goes in v7:
time: 113 us
  blocking collectives  54.6 us (48%)
  local copies, waits for them, and re-layouts  23 us (20%)
  Pallas kernels  18.2 us (16%)
  starting transfers between devices  7.48 us (7%)
  waiting for transfers between devices  4.09 us (4%)
  other arithmetic  3.92 us (3%)
    all_to_all x1, blocking collectives, on_device(): lax.all_to_all(outgoing, 'node', split_axis=0, concat_axis=0, tiled=True)  54.6 us
    pallas_call x1, Pallas kernels, hist_and_best(): pl.pallas_call(histogram_kernel, grid_spec=pltpu.PrefetchScalarGridSpec(n...  18.2 us
    scatter x1, local copies, waits for them, and re-layouts, on_device(): outgoing = empty.T.at[position].set(payload.T, mode='drop')  12 us
    all_to_all x1, starting transfers between devices, on_device(): lax.all_to_all(spread, 'feat', split_axis=0, concat_axis=0, tiled=True)  7.48 us
    all_to_all x1, waiting for transfers between devices, on_device(): lax.all_to_all(spread, 'feat', split_axis=0, concat_axis=0, tiled=True)  4.09 us
    reshape x2, local copies, waits for them, and re-layouts, on_device(): jnp.transpose(arrived, (1, 3, 2, 0))  3.2 us
  transfers between devices with their start and end apart: 1, of which 1 were waited for; matrix products, arithmetic and copies ran while one was open for 2% of the time, Pallas kernels for 0%

profile of v7, /device:TPU:2, one launch (start us, length us, event | category | flops | bytes accessed | tf_op | source)
XLA Modules:
  0.0 112.6 jit_solution(17617610580383947728)
XLA Ops:
  0.6 0.7 broadcast_compare_fusion
  1.4 1.0 select_reduce_fusion
  2.4 0.1 pad.2.clone
  2.4 1.1 maximum_bitcast_fusion
  3.5 0.0 copy-start
  3.5 0.5 copy.26
  4.0 0.4 convolution_bitcast_fusion
  4.4 0.4 slice_reduce_fusion
  4.8 0.1 fusion.5
  4.9 0.4 multiply_reduce_fusion
  5.3 0.0 copy-done
  5.4 0.3 transpose.19
  5.7 12.0 %scatter_fusion = bf16[8192,33]{1,0:T(8,128)(2,1)S(1)} fusion(bf16[8192,33]{1,0:T(8,128)(2,1)S(1)} %transpose.19, s32[4096]{0:T(1024)S(1)} %compare_select_fusion, bf16[4096,33]{1,0:T(8,128)(2,1)S(1)} %copy.26), kind=kCustom, calls=%fused_computation | custom fusion | bytes 827392 | tf_op jit(solution)/shard_map/scatter | solution.py:108
  17.6 1.0 copy.27
  18.6 54.6 %all_to_all.11 = bf16[32,256,33]{1,2,0:T(8,128)(2,1)S(1)} all-to-all(bf16[32,256,33]{1,2,0:T(8,128)(2,1)S(1)} %copy.27), channel_id=1, replica_groups=mesh['node'=32,'feat'=16] {'node'}, dimensions={0} | all-to-all | bytes 1081344 | tf_op jit(solution)/shard_map/all_to_all | solution.py:110
  73.3 0.3 reshape.63
  73.6 1.2 %copy.29 = bf16[2,33,128,32]{3,2,0,1:T(8,128)(2,1)S(1)} copy(bf16[2,33,128,32]{2,0,1,3:T(2,128)(2,1)S(1)} %bitcast.29) | data formatting | bytes 1081344 | tf_op jit(solution)/shard_map/transpose | solution.py:112
  74.8 2.1 %reshape.51 = bf16[2,33,4096]{2,0,1:T(2,128)(2,1)S(1)} reshape(bf16[2,33,128,32]{3,2,0,1:T(8,128)(2,1)S(1)} %copy.29) | data formatting | bytes 1081344 | tf_op jit(solution)/shard_map/reshape | solution.py:112
  76.9 1.1 %copy.30.rows_ref = bf16[2,33,4096]{2,1,0:T(8,128)(2,1)} copy(bf16[2,33,4096]{2,0,1:T(2,128)(2,1)S(1)} %reshape.51) | data formatting | bytes 1081344 | tf_op jit(solution)/shard_map/reshape | solution.py:112
  78.0 0.1 bitcast_reduce_fusion
  78.2 0.6 reshape.52.flags_ref
  78.8 18.2 %shard_map.68 = (f32[2,16,17,256]{3,2,1,0:T(8,128)}, f32[2,8,128]{2,1,0:T(8,128)}) custom-call(s32[16]{0:T(128)} %reshape.52.flags_ref, bf16[2,33,4096]{2,1,0:T(8,128)(2,1)} %copy.30.rows_ref), custom_call_target="tpu_custom_call" | custom-call | tf_op jit(solution)/shard_map/pallas_call | solution.py:56
  96.9 0.8 slice_reduce_fusion.1
  97.7 0.6 broadcast_in_dim.30
  98.3 7.5 %all-to-all-start.1 = ((f32[16,1,2]{2,1,0:T(1,128)}), f32[16,1,2]{2,1,0:T(1,128)S(1)}, u32[]{:S(2)}, u32[]{:S(2)}) async-start(f32[16,1,2]{2,1,0:T(1,128)} %broadcast_in_dim.30), calls=%async_computation.1 | async-start | bytes 16384 | tf_op jit(solution)/shard_map/all_to_all | solution.py:115
  105.8 2.1 %copy.32 = f32[2,16,17,256]{3,1,2,0:T(8,128)} copy(f32[2,16,17,256]{3,2,1,0:T(8,128)} %get-tuple-element.14) | data formatting | bytes 1114112
  107.9 4.1 %all-to-all-done.1 = f32[16,1,2]{2,1,0:T(1,128)S(1)} async-done(((f32[16,1,2]{2,1,0:T(1,128)}), f32[16,1,2]{2,1,0:T(1,128)S(1)}, u32[]{:S(2)}, u32[]{:S(2)}) %all-to-all-start.1) | async-done | bytes 160 | tf_op jit(solution)/shard_map/all_to_all | solution.py:115
  112.0 0.5 reduce_max.9
  (9 shorter events, 0.1 us)
Async XLA Ops:
  3.5 1.8 %copy-start = (s32[4096]{0:T(1024)S(1)}, s32[4096]{0:T(1024)}, u32[]{:S(2)}) copy-start(s32[4096]{0:T(1024)} %param.7) | copy-start | bytes 49156
  98.3 13.7 %all-to-all-start.1 = ((f32[16,1,2]{2,1,0:T(1,128)}), f32[16,1,2]{2,1,0:T(1,128)S(1)}, u32[]{:S(2)}, u32[]{:S(2)}) async-start(f32[16,1,2]{2,1,0:T(1,128)} %broadcast_in_dim.30), calls=%async_computation.1 | async-start | bytes 16384 | tf_op jit(solution)/shard_map/all_to_all | solution.py:115

commit v8 on v6

--- a/solution.py
+++ b/solution.py
@@ -7,7 +7,7 @@
 
 B = 256
 BLOCK = 256
-CH = 512
+CH = 256
 
 
 def histogram_kernel(flags_ref, bins_ref, stats_ref, hist_ref, best_ref):

time: 109 us -> 104 us (0.954)
  Pallas kernels: 19.4 us -> 13.4 us
    pallas_call x1, Pallas kernels: 19.4 us -> 13.4 us  [hist_and_best(): pl.pallas_call(histogram_kernel, grid_spec=pltpu.PrefetchScalarGridSpec(n...]
where the time goes in v8:
time: 104 us; the launch traced here: 103 us
  blocking collectives  50.1 us (48%)
  local copies, waits for them, and re-layouts  22.8 us (22%)
  Pallas kernels  13.4 us (13%)
  starting transfers between devices  6.76 us (6%)
  waiting for transfers between devices  4.3 us (4%)
  other arithmetic  3.96 us (4%)
    all_to_all x1, blocking collectives, on_device(): lax.all_to_all(outgoing, 'node', split_axis=0, concat_axis=0, tiled=True)  50.1 us
    pallas_call x1, Pallas kernels, hist_and_best(): pl.pallas_call(histogram_kernel, grid_spec=pltpu.PrefetchScalarGridSpec(n...  13.4 us
    scatter x1, local copies, waits for them, and re-layouts, on_device(): outgoing = empty.T.at[position].set(payload.T, mode='drop')  12 us
    all_to_all x1, starting transfers between devices, on_device(): lax.all_to_all(spread, 'feat', split_axis=0, concat_axis=0, tiled=True)  6.76 us
    all_to_all x1, waiting for transfers between devices, on_device(): lax.all_to_all(spread, 'feat', split_axis=0, concat_axis=0, tiled=True)  4.3 us
    unnamed x6, local copies, waits for them, and re-layouts  2.13 us
  transfers between devices with their start and end apart: 1, of which 1 were waited for; matrix products, arithmetic and copies ran while one was open for 2% of the time, Pallas kernels for 0%

profile of v8, /device:TPU:1, one launch (start us, length us, event | category | flops | bytes accessed | tf_op | source)
XLA Modules:
  0.0 102.6 jit_solution(240409740504897474)
XLA Ops:
  0.6 0.7 broadcast_compare_fusion
  1.4 1.0 select_reduce_fusion
  2.4 1.0 maximum_bitcast_fusion
  3.3 0.0 copy-start.1
  3.4 0.5 copy.25
  3.8 0.4 convolution_bitcast_fusion
  4.2 0.4 slice_reduce_fusion
  4.6 0.1 fusion.5
  4.7 0.4 multiply_reduce_fusion
  5.2 0.0 copy-done.1
  5.2 0.3 transpose.25
  5.5 12.0 %scatter_fusion = bf16[8192,32]{1,0:T(8,128)(2,1)S(1)} fusion(bf16[8192,32]{1,0:T(8,128)(2,1)S(1)} %transpose.25, s32[4096]{0:T(1024)S(1)} %compare_select_fusion, bf16[4096,32]{1,0:T(8,128)(2,1)S(1)} %copy.25), kind=kCustom, calls=%fused_computation | custom fusion | bytes 802816 | tf_op jit(solution)/shard_map/scatter | solution.py:107
  17.5 0.8 copy.26
  18.3 50.1 %all_to_all.11 = bf16[32,256,32]{1,2,0:T(8,128)(2,1)S(1)} all-to-all(bf16[32,256,32]{1,2,0:T(8,128)(2,1)S(1)} %copy.26), channel_id=1, replica_groups=mesh['node'=32,'feat'=16] {'node'}, dimensions={0} | all-to-all | bytes 1048576 | tf_op jit(solution)/shard_map/all_to_all | solution.py:109
  68.3 0.1 reshape.55
  68.5 0.6 copy.37
  69.1 0.1 floor_convert_fusion
  69.2 0.5 copy.29
  69.7 1.1 %slice.23 = bf16[16,2,4096]{2,0,1:T(8,128)(2,1)S(1)} reshape(bf16[16,2,128,32]{3,2,0,1:T(8,128)(2,1)S(1)} %copy.29) | data formatting | bytes 524288 | tf_op jit(solution)/shard_map/slice | solution.py:115
  70.8 0.8 concatenate.11.stats_ref
  71.6 0.6 copy.28
  72.3 1.0 convert_element_type.40
  73.2 0.0 copy-start
  73.2 0.1 compare_reduce_fusion
  73.3 0.1 bitcast_reduce_fusion
  73.4 0.6 reshape.56.flags_ref
  74.0 0.0 copy-done
  74.0 13.4 %shard_map.68 = (f32[2,16,17,256]{3,2,1,0:T(8,128)}, f32[2,8,128]{2,1,0:T(8,128)}) custom-call(s32[32]{0:T(128)} %reshape.56.flags_ref, s32[2,16,4096]{2,1,0:T(8,128)} %bitcast.34, bf16[2,17,4096]{2,1,0:T(8,128)(2,1)} %concatenate.11.stats_ref), custom_call_target="tpu_custom_call" | custom-call | tf_op jit(solution)/shard_map/pallas_call | solution.py:55
  87.5 0.8 slice_reduce_fusion.1
  88.3 0.6 broadcast_in_dim.27
  88.9 6.8 %all-to-all-start.1 = ((f32[16,1,2]{2,1,0:T(1,128)}), f32[16,1,2]{2,1,0:T(1,128)S(1)}, u32[]{:S(2)}, u32[]{:S(2)}) async-start(f32[16,1,2]{2,1,0:T(1,128)} %broadcast_in_dim.27), calls=%async_computation.1 | async-start | bytes 16384 | tf_op jit(solution)/shard_map/all_to_all | solution.py:118
  95.6 2.1 %copy.31 = f32[2,16,17,256]{3,1,2,0:T(8,128)} copy(f32[2,16,17,256]{3,2,1,0:T(8,128)} %get-tuple-element.14) | data formatting | bytes 1114112
  97.7 4.3 %all-to-all-done.1 = f32[16,1,2]{2,1,0:T(1,128)S(1)} async-done(((f32[16,1,2]{2,1,0:T(1,128)}), f32[16,1,2]{2,1,0:T(1,128)S(1)}, u32[]{:S(2)}, u32[]{:S(2)}) %all-to-all-start.1) | async-done | bytes 160 | tf_op jit(solution)/shard_map/all_to_all | solution.py:118
  102.0 0.5 reduce_max.9
  (9 shorter events, 0.1 us)
Async XLA Ops:
  3.3 1.8 %copy-start.1 = (s32[4096]{0:T(1024)S(1)}, s32[4096]{0:T(1024)}, u32[]{:S(2)}) copy-start(s32[4096]{0:T(1024)} %param.7) | copy-start | bytes 49156
  73.2 0.8 copy-start
  88.9 13.2 %all-to-all-start.1 = ((f32[16,1,2]{2,1,0:T(1,128)}), f32[16,1,2]{2,1,0:T(1,128)S(1)}, u32[]{:S(2)}, u32[]{:S(2)}) async-start(f32[16,1,2]{2,1,0:T(1,128)} %broadcast_in_dim.27), calls=%async_computation.1 | async-start | bytes 16384 | tf_op jit(solution)/shard_map/all_to_all | solution.py:118

commit v9 on v8

--- a/solution.py
+++ b/solution.py
@@ -7,7 +7,8 @@
 
 B = 256
 BLOCK = 256
-CH = 256
+CH = 128
+GROUPS = 4
 
 
 def histogram_kernel(flags_ref, bins_ref, stats_ref, hist_ref, best_ref):
@@ -19,17 +20,20 @@
     levels = lax.broadcasted_iota(jnp.int32, (B, CH), 0)
     best = jnp.full((1, B), -jnp.inf, jnp.float32)
     hist_ref[...] = jnp.zeros(hist_ref.shape, hist_ref.dtype)
-    for k in range(chunks):
-
+    def chunk(k, carry):
         @pl.when(flags_ref[node * chunks + k] > 0)
         def _():
+            offset = pl.multiple_of(k * CH, CH)
+            stats = stats_ref[0, :, pl.ds(offset, CH)]
             for f in range(feats):
-                row = bins_ref[0, f:f + 1, k * CH:(k + 1) * CH]
+                row = bins_ref[0, f:f + 1, pl.ds(offset, CH)]
                 indicator = (levels == row).astype(jnp.bfloat16)
                 hist_ref[0, f] += lax.dot_general(
-                    stats_ref[0, :, k * CH:(k + 1) * CH], indicator, (((1,), (1,)), ((), ())),
-                    preferred_element_type=jnp.float32)
+                    stats, indicator, (((1,), (1,)), ((), ())), preferred_element_type=jnp.float32)
 
+        return carry
+
+    lax.fori_loop(0, chunks, chunk, 0)
     lane = lax.broadcasted_iota(jnp.int32, (stat_count, B), 1)
     for f in range(feats):
         left = hist_ref[0, f]
@@ -107,8 +111,8 @@
     outgoing = empty.T.at[position].set(payload.T, mode="drop")
     outgoing = outgoing.reshape(node_devices, node_local * capacity, payload_width)
     arrived = lax.all_to_all(outgoing, "node", split_axis=0, concat_axis=0, tiled=True)
-    arrived = arrived.reshape(node_devices, node_local, capacity, payload_width)
-    arrived = jnp.transpose(arrived, (3, 1, 2, 0)).reshape(payload_width, node_local, capacity * node_devices)
+    arrived = arrived.reshape(GROUPS, node_devices // GROUPS, node_local, capacity, payload_width)
+    arrived = jnp.transpose(arrived, (4, 2, 0, 3, 1)).reshape(payload_width, node_local, capacity * node_devices)
     bin_table = jnp.floor(arrived[:feat_count].astype(jnp.float32) * B).astype(jnp.int32)
     bin_table = jnp.transpose(bin_table, (1, 0, 2))
     ones = jnp.ones((node_local, 1, arrived.shape[2]), jnp.bfloat16)

time: 104 us -> 119 us (1.14)
  Pallas kernels: 13.4 us -> 24.8 us
  local copies, waits for them, and re-layouts: 22.8 us -> 27 us
    pallas_call x1, Pallas kernels: 13.4 us -> 24.8 us  [hist_and_best(): pl.pallas_call(histogram_kernel, grid_spec=pltpu.PrefetchScalarGridSpec(n...]
    convert_element_type x2, local copies, waits for them, and re-layouts: 1.55 us -> 5.38 us  [on_device(): jnp.floor(arrived[:feat_count].astype(jnp.float32) * B).astype(jnp.int32)]
where the time goes in v9:
time: 119 us; the launch traced here: 118 us
  blocking collectives  50.1 us (42%)
  local copies, waits for them, and re-layouts  27 us (23%)
  Pallas kernels  24.8 us (21%)
  starting transfers between devices  6.75 us (6%)
  waiting for transfers between devices  4.3 us (4%)
  other arithmetic  3.96 us (3%)
    all_to_all x1, blocking collectives, on_device(): lax.all_to_all(outgoing, 'node', split_axis=0, concat_axis=0, tiled=True)  50.1 us
    pallas_call x1, Pallas kernels, hist_and_best(): pl.pallas_call(histogram_kernel, grid_spec=pltpu.PrefetchScalarGridSpec(n...  24.8 us
    scatter x1, local copies, waits for them, and re-layouts, on_device(): outgoing = empty.T.at[position].set(payload.T, mode='drop')  12 us
    all_to_all x1, starting transfers between devices, on_device(): lax.all_to_all(spread, 'feat', split_axis=0, concat_axis=0, tiled=True)  6.75 us
    convert_element_type x2, local copies, waits for them, and re-layouts, on_device(): jnp.floor(arrived[:feat_count].astype(jnp.float32) * B).astype(jnp.int32)  5.38 us
    all_to_all x1, waiting for transfers between devices, on_device(): lax.all_to_all(spread, 'feat', split_axis=0, concat_axis=0, tiled=True)  4.3 us
  transfers between devices with their start and end apart: 1, of which 1 were waited for; matrix products, arithmetic and copies ran while one was open for 2% of the time, Pallas kernels for 0%

profile of v9, /device:TPU:1, one launch (start us, length us, event | category | flops | bytes accessed | tf_op | source)
XLA Modules:
  0.0 118.2 jit_solution(677342280090290026)
XLA Ops:
  0.6 0.7 broadcast_compare_fusion
  1.4 1.0 select_reduce_fusion
  2.4 1.0 maximum_bitcast_fusion
  3.3 0.0 copy-start.1
  3.4 0.5 copy.31
  3.8 0.4 convolution_bitcast_fusion
  4.2 0.4 slice_reduce_fusion
  4.6 0.1 fusion.5
  4.7 0.4 multiply_reduce_fusion
  5.2 0.0 copy-done.1
  5.2 0.3 transpose.25
  5.5 12.0 %scatter_fusion = bf16[8192,32]{1,0:T(8,128)(2,1)S(1)} fusion(bf16[8192,32]{1,0:T(8,128)(2,1)S(1)} %transpose.25, s32[4096]{0:T(1024)S(1)} %compare_select_fusion, bf16[4096,32]{1,0:T(8,128)(2,1)S(1)} %copy.31), kind=kCustom, calls=%fused_computation | custom fusion | bytes 802816 | tf_op jit(solution)/shard_map/scatter | solution.py:111
  17.5 0.8 copy.32
  18.3 50.1 %all_to_all.11 = bf16[32,256,32]{1,2,0:T(8,128)(2,1)S(1)} all-to-all(bf16[32,256,32]{1,2,0:T(8,128)(2,1)S(1)} %copy.32), channel_id=1, replica_groups=mesh['node'=32,'feat'=16] {'node'}, dimensions={0} | all-to-all | bytes 1048576 | tf_op jit(solution)/shard_map/all_to_all | solution.py:113
  68.3 0.1 reshape.55
  68.5 0.6 copy.45
  69.1 0.1 floor_convert_fusion
  69.2 1.2 %copy.36 = bf16[16,2,4,128,8]{0,4,3,2,1:T(8,128)(2,1)S(1)} copy(bf16[16,2,4,128,8]{3,4,2,1,0:T(8,128)(2,1)S(1)} %slice.28) | data formatting | bytes 524288 | tf_op jit(solution)/shard_map/slice | solution.py:119
  70.4 0.8 copy.37
  71.2 0.8 concatenate.11.stats_ref
  72.1 2.6 %copy.34 = s32[16,2,4,128,8]{0,4,3,2,1:T(8,128)} copy(s32[16,2,4,128,8]{3,4,2,1,0:T(8,128)S(1)} %floor_convert_fusion) | data formatting | bytes 1048576 | tf_op jit(solution)/shard_map/convert_element_type | solution.py:116
  74.7 2.8 %copy.35 = s32[16,2,4096]{2,0,1:T(8,128)S(1)} copy(s32[16,2,4096]{0,2,1:T(8,128)} %bitcast.27) | data formatting | bytes 1048576 | tf_op jit(solution)/shard_map/convert_element_type | solution.py:116
  77.5 0.0 copy-start
  77.5 0.1 compare_reduce_fusion
  77.6 0.1 bitcast_reduce_fusion
  77.7 0.6 reshape.56.flags_ref
  78.3 0.0 copy-done
  78.3 24.8 %shard_map.68 = (f32[2,16,17,256]{3,2,1,0:T(8,128)}, f32[2,8,128]{2,1,0:T(8,128)}) custom-call(s32[64]{0:T(128)} %reshape.56.flags_ref, s32[2,16,4096]{2,1,0:T(8,128)} %bitcast.30, bf16[2,17,4096]{2,1,0:T(8,128)(2,1)} %concatenate.11.stats_ref), custom_call_target="tpu_custom_call" | custom-call | tf_op jit(solution)/shard_map/pallas_call | solution.py:59
  103.1 0.8 slice_reduce_fusion.1
  103.9 0.6 broadcast_in_dim.27
  104.5 6.8 %all-to-all-start.1 = ((f32[16,1,2]{2,1,0:T(1,128)}), f32[16,1,2]{2,1,0:T(1,128)S(1)}, u32[]{:S(2)}, u32[]{:S(2)}) async-start(f32[16,1,2]{2,1,0:T(1,128)} %broadcast_in_dim.27), calls=%async_computation.1 | async-start | bytes 16384 | tf_op jit(solution)/shard_map/all_to_all | solution.py:122
  111.2 2.1 %copy.39 = f32[2,16,17,256]{3,1,2,0:T(8,128)} copy(f32[2,16,17,256]{3,2,1,0:T(8,128)} %get-tuple-element.14) | data formatting | bytes 1114112
  113.4 4.3 %all-to-all-done.1 = f32[16,1,2]{2,1,0:T(1,128)S(1)} async-done(((f32[16,1,2]{2,1,0:T(1,128)}), f32[16,1,2]{2,1,0:T(1,128)S(1)}, u32[]{:S(2)}, u32[]{:S(2)}) %all-to-all-start.1) | async-done | bytes 160 | tf_op jit(solution)/shard_map/all_to_all | solution.py:122
  117.7 0.5 reduce_max.9
  (9 shorter events, 0.1 us)
Async XLA Ops:
  3.3 1.8 %copy-start.1 = (s32[4096]{0:T(1024)S(1)}, s32[4096]{0:T(1024)}, u32[]{:S(2)}) copy-start(s32[4096]{0:T(1024)} %param.7) | copy-start | bytes 49156
  77.5 0.8 copy-start
  104.5 13.2 %all-to-all-start.1 = ((f32[16,1,2]{2,1,0:T(1,128)}), f32[16,1,2]{2,1,0:T(1,128)S(1)}, u32[]{:S(2)}, u32[]{:S(2)}) async-start(f32[16,1,2]{2,1,0:T(1,128)} %broadcast_in_dim.27), calls=%async_computation.1 | async-start | bytes 16384 | tf_op jit(solution)/shard_map/all_to_all | solution.py:122

commit v10 on v8

--- a/solution.py
+++ b/solution.py
@@ -16,7 +16,7 @@
     stat_count = stats_ref.shape[1]
     chunks = slots // CH
     node = pl.program_id(0)
-    levels = lax.broadcasted_iota(jnp.int32, (B, CH), 0)
+    levels = lax.broadcasted_iota(jnp.int32, (B, CH), 0).astype(jnp.float32)
     best = jnp.full((1, B), -jnp.inf, jnp.float32)
     hist_ref[...] = jnp.zeros(hist_ref.shape, hist_ref.dtype)
     for k in range(chunks):
@@ -24,7 +24,7 @@
         @pl.when(flags_ref[node * chunks + k] > 0)
         def _():
             for f in range(feats):
-                row = bins_ref[0, f:f + 1, k * CH:(k + 1) * CH]
+                row = bins_ref[0, f:f + 1, k * CH:(k + 1) * CH].astype(jnp.float32)
                 indicator = (levels == row).astype(jnp.bfloat16)
                 hist_ref[0, f] += lax.dot_general(
                     stats_ref[0, :, k * CH:(k + 1) * CH], indicator, (((1,), (1,)), ((), ())),
@@ -44,9 +44,9 @@
         right_part = jnp.sum(right[1:] * right[1:], axis=0, keepdims=True) / (right[0:1] + 1.0)
         total_part = jnp.sum(total[1:] * total[1:], axis=0, keepdims=True) / (total[0:1] + 1.0)
         best = jnp.maximum(best, left_part + right_part - total_part)
-    best_ref[0] = jnp.broadcast_to(jnp.max(best, axis=1, keepdims=True), (8, 128))
+    best_ref[0] = jnp.broadcast_to(jnp.max(best, axis=1, keepdims=True), best_ref.shape[1:])
 
-def hist_and_best(bins, stats):
+def hist_and_best(bins, stats, spread):
     nodes, feats, slots = bins.shape
     st = stats.shape[1]
     chunks = slots // CH
@@ -60,10 +60,10 @@
             in_specs=[pl.BlockSpec((1, feats, slots), lambda n, fl: (n, 0, 0)),
                       pl.BlockSpec((1, st, slots), lambda n, fl: (n, 0, 0))],
             out_specs=[pl.BlockSpec((1, feats, st, B), lambda n, fl: (n, 0, 0, 0)),
-                       pl.BlockSpec((1, 8, 128), lambda n, fl: (n, 0, 0))]),
+                       pl.BlockSpec((1, spread, 128), lambda n, fl: (n, 0, 0))]),
         out_shape=[jax.ShapeDtypeStruct((nodes, feats, st, B), jnp.float32),
-                   jax.ShapeDtypeStruct((nodes, 8, 128), jnp.float32)])(flags, bins, stats)
-    return hist, best[:, 0, 0]
+                   jax.ShapeDtypeStruct((nodes, spread, 128), jnp.float32)])(flags, bins, stats)
+    return hist, best
 
 
 def running_rank(owned):
@@ -109,14 +109,13 @@
     arrived = lax.all_to_all(outgoing, "node", split_axis=0, concat_axis=0, tiled=True)
     arrived = arrived.reshape(node_devices, node_local, capacity, payload_width)
     arrived = jnp.transpose(arrived, (3, 1, 2, 0)).reshape(payload_width, node_local, capacity * node_devices)
-    bin_table = jnp.floor(arrived[:feat_count].astype(jnp.float32) * B).astype(jnp.int32)
+    bin_table = jnp.floor(arrived[:feat_count] * B)
     bin_table = jnp.transpose(bin_table, (1, 0, 2))
     ones = jnp.ones((node_local, 1, arrived.shape[2]), jnp.bfloat16)
     statistics = jnp.concatenate([ones, jnp.transpose(arrived[feat_count:], (1, 0, 2))], axis=1)
-    histogram, best_local = hist_and_best(bin_table, statistics)
-    spread = jnp.broadcast_to(best_local[None, :], (feat_devices, node_local))
-    gathered = lax.all_to_all(spread, "feat", split_axis=0, concat_axis=0, tiled=True)
-    best_gain = jnp.max(gathered, axis=0)
+    histogram, best_spread = hist_and_best(bin_table, statistics, feat_devices)
+    gathered = lax.all_to_all(best_spread, "feat", split_axis=1, concat_axis=1, tiled=True)
+    best_gain = jnp.max(gathered[:, :, 0], axis=1)
     return (histogram, best_gain)
 
 

time: 104 us -> 106 us (1.019)
  Pallas kernels: 13.4 us -> 16.3 us
    pallas_call x1, Pallas kernels: 13.4 us -> 16.3 us  [hist_and_best(): pl.pallas_call(histogram_kernel, grid_spec=pltpu.PrefetchScalarGridSpec(n...]
    floor x0 -> x2, local copies, waits for them, and re-layouts: none -> 1.75 us  [on_device(): bin_table = jnp.floor(arrived[:feat_count] * B)]
    convert_element_type x2 -> x0, local copies, waits for them, and re-layouts: 1.55 us -> none  [on_device(): jnp.floor(arrived[:feat_count].astype(jnp.float32) * B).astype(jnp.int32)]
    pallas_call x0 -> x1, local copies, waits for them, and re-layouts: none -> 1.32 us  [hist_and_best(): pl.pallas_call(histogram_kernel, grid_spec=pltpu.PrefetchScalarGridSpec(n...]
where the time goes in v10:
time: 106 us
  blocking collectives  50.1 us (47%)
  local copies, waits for them, and re-layouts  22.4 us (21%)
  Pallas kernels  16.3 us (15%)
  starting transfers between devices  6.76 us (6%)
  other arithmetic  4.41 us (4%)
  waiting for transfers between devices  4.34 us (4%)
    all_to_all x1, blocking collectives, on_device(): lax.all_to_all(outgoing, 'node', split_axis=0, concat_axis=0, tiled=True)  50.1 us
    pallas_call x1, Pallas kernels, hist_and_best(): pl.pallas_call(histogram_kernel, grid_spec=pltpu.PrefetchScalarGridSpec(n...  16.3 us
    scatter x1, local copies, waits for them, and re-layouts, on_device(): outgoing = empty.T.at[position].set(payload.T, mode='drop')  12 us
    all_to_all x1, starting transfers between devices, on_device(): lax.all_to_all(best_spread, 'feat', split_axis=1, concat_axis=1, tiled=True)  6.76 us
    all_to_all x1, waiting for transfers between devices, on_device(): lax.all_to_all(best_spread, 'feat', split_axis=1, concat_axis=1, tiled=True)  4.34 us
    unnamed x6, local copies, waits for them, and re-layouts  2.13 us
  transfers between devices with their start and end apart: 1, of which 1 were waited for; matrix products, arithmetic and copies ran while one was open for 2% of the time, Pallas kernels for 0%

profile of v10, /device:TPU:1, one launch (start us, length us, event | category | flops | bytes accessed | tf_op | source)
XLA Modules:
  0.0 105.6 jit_solution(8471143009091114592)
XLA Ops:
  0.6 0.7 broadcast_compare_fusion
  1.4 1.0 select_reduce_fusion
  2.4 1.0 maximum_bitcast_fusion
  3.3 0.0 copy-start.1
  3.4 0.5 copy.20
  3.8 0.4 convolution_bitcast_fusion
  4.2 0.4 slice_reduce_fusion
  4.6 0.1 fusion.6
  4.7 0.4 multiply_reduce_fusion
  5.2 0.0 copy-done.1
  5.2 0.3 transpose.24
  5.5 12.0 %scatter_fusion = bf16[8192,32]{1,0:T(8,128)(2,1)S(1)} fusion(bf16[8192,32]{1,0:T(8,128)(2,1)S(1)} %transpose.24, s32[4096]{0:T(1024)S(1)} %compare_select_fusion, bf16[4096,32]{1,0:T(8,128)(2,1)S(1)} %copy.20), kind=kCustom, calls=%fused_computation | custom fusion | bytes 802816 | tf_op jit(solution)/shard_map/scatter | solution.py:107
  17.5 0.8 copy.21
  18.3 50.1 %all_to_all.10 = bf16[32,256,32]{1,2,0:T(8,128)(2,1)S(1)} all-to-all(bf16[32,256,32]{1,2,0:T(8,128)(2,1)S(1)} %copy.21), channel_id=1, replica_groups=mesh['node'=32,'feat'=16] {'node'}, dimensions={0} | all-to-all | bytes 1048576 | tf_op jit(solution)/shard_map/all_to_all | solution.py:109
  68.3 0.1 reshape.45
  68.5 0.4 fusion.7
  68.9 0.7 copy.23
  69.6 1.1 %slice.23 = bf16[16,2,4096]{2,0,1:T(8,128)(2,1)S(1)} reshape(bf16[16,2,128,32]{3,2,0,1:T(8,128)(2,1)S(1)} %copy.23) | data formatting | bytes 524288 | tf_op jit(solution)/shard_map/slice | solution.py:115
  70.7 0.8 concatenate.11.stats_ref
  71.5 0.6 copy.22
  72.2 1.1 %floor.7 = bf16[16,2,4096]{2,0,1:T(8,128)(2,1)S(1)} reshape(bf16[16,2,128,32]{3,2,0,1:T(8,128)(2,1)S(1)} %copy.22) | data formatting | bytes 524288 | tf_op jit(solution)/shard_map/floor | solution.py:112
  73.3 0.0 copy-start
  73.3 0.1 compare_reduce_fusion
  73.4 0.1 bitcast_reduce_fusion
  73.5 0.6 reshape.46.flags_ref
  74.1 0.0 copy-done
  74.1 16.3 %shard_map.68 = (f32[2,16,17,256]{3,2,1,0:T(8,128)}, f32[2,16,128]{2,1,0:T(8,128)}) custom-call(s32[32]{0:T(128)} %reshape.46.flags_ref, bf16[2,16,4096]{2,1,0:T(8,128)(2,1)} %bitcast.33, bf16[2,17,4096]{2,1,0:T(8,128)(2,1)} %concatenate.11.stats_ref), custom_call_target="tpu_custom_call" | custom-call | tf_op jit(solution)/shard_map/pallas_call | solution.py:55
  90.4 1.3 %copy.24 = f32[2,16,128]{2,0,1:T(2,128)} copy(f32[2,16,128]{2,1,0:T(8,128)} %get-tuple-element.5) | data formatting | bytes 32768 | tf_op jit(solution)/shard_map/pallas_call | solution.py:55
  91.7 6.8 %all-to-all-start.1 = ((f32[2,16,128]{2,0,1:T(2,128)}), f32[2,16,128]{2,0,1:T(2,128)S(1)}, u32[]{:S(2)}, u32[]{:S(2)}) async-start(f32[2,16,128]{2,0,1:T(2,128)} %copy.24), calls=%async_computation.1 | async-start | bytes 32768 | tf_op jit(solution)/shard_map/all_to_all | solution.py:117
  98.5 2.1 %copy.25 = f32[2,16,17,256]{3,1,2,0:T(8,128)} copy(f32[2,16,17,256]{3,2,1,0:T(8,128)} %get-tuple-element.12) | data formatting | bytes 1114112
  100.6 4.3 %all-to-all-done.1 = f32[2,16,128]{2,0,1:T(2,128)S(1)} async-done(((f32[2,16,128]{2,0,1:T(2,128)}), f32[2,16,128]{2,0,1:T(2,128)S(1)}, u32[]{:S(2)}, u32[]{:S(2)}) %all-to-all-start.1) | async-done | bytes 16416 | tf_op jit(solution)/shard_map/all_to_all | solution.py:117
  105.0 0.6 slice_reduce_fusion.1
  (8 shorter events, 0.1 us)
Async XLA Ops:
  3.3 1.8 %copy-start.1 = (s32[4096]{0:T(1024)S(1)}, s32[4096]{0:T(1024)}, u32[]{:S(2)}) copy-start(s32[4096]{0:T(1024)} %param.7) | copy-start | bytes 49156
  73.3 0.9 copy-start
  91.7 13.2 %all-to-all-start.1 = ((f32[2,16,128]{2,0,1:T(2,128)}), f32[2,16,128]{2,0,1:T(2,128)S(1)}, u32[]{:S(2)}, u32[]{:S(2)}) async-start(f32[2,16,128]{2,0,1:T(2,128)} %copy.24), calls=%async_computation.1 | async-start | bytes 32768 | tf_op jit(solution)/shard_map/all_to_all | solution.py:117

commit v11 on v10

--- a/solution.py
+++ b/solution.py
@@ -99,17 +99,17 @@
     rank = running_rank(owned)
     slots = node_total * capacity
     position = jnp.where(kept, target * capacity + rank, slots)
-    payload = jnp.concatenate([covariates, pseudo], axis=0)
+    payload = jnp.concatenate([jnp.floor(covariates * B), pseudo], axis=0)
     payload_width = payload.shape[0]
     empty = jnp.concatenate(
-        [jnp.ones((feat_count, slots), jnp.bfloat16), jnp.zeros((payload_width - feat_count, slots), jnp.bfloat16)]
+        [jnp.full((feat_count, slots), B, jnp.bfloat16), jnp.zeros((payload_width - feat_count, slots), jnp.bfloat16)]
     )
     outgoing = empty.T.at[position].set(payload.T, mode="drop")
     outgoing = outgoing.reshape(node_devices, node_local * capacity, payload_width)
     arrived = lax.all_to_all(outgoing, "node", split_axis=0, concat_axis=0, tiled=True)
     arrived = arrived.reshape(node_devices, node_local, capacity, payload_width)
     arrived = jnp.transpose(arrived, (3, 1, 2, 0)).reshape(payload_width, node_local, capacity * node_devices)
-    bin_table = jnp.floor(arrived[:feat_count] * B)
+    bin_table = arrived[:feat_count]
     bin_table = jnp.transpose(bin_table, (1, 0, 2))
     ones = jnp.ones((node_local, 1, arrived.shape[2]), jnp.bfloat16)
     statistics = jnp.concatenate([ones, jnp.transpose(arrived[feat_count:], (1, 0, 2))], axis=1)

time: 106 us -> 106 us (level); the launches traced: 106 us -> 104 us
  Pallas kernels: 16.3 us -> 13.4 us
    pallas_call x1, Pallas kernels: 16.3 us -> 13.4 us  [hist_and_best(): pl.pallas_call(histogram_kernel, grid_spec=pltpu.PrefetchScalarGridSpec(n...]
    slice x0 -> x2, local copies, waits for them, and re-layouts: none -> 1.76 us  [on_device(): bin_table = arrived[:feat_count]]
    floor x2 -> x0, local copies, waits for them, and re-layouts: 1.75 us -> none  [on_device(): bin_table = jnp.floor(arrived[:feat_count] * B)]
    slice x2 -> x3, local copies, waits for them, and re-layouts: 1.76 us -> 2.13 us  [on_device(): arrived[feat_count:]]
where the time goes in v11:
time: 106 us; the launch traced here: 104 us
  blocking collectives  50.1 us (47%)
  local copies, waits for them, and re-layouts  22.8 us (22%)
  Pallas kernels  13.4 us (13%)
  starting transfers between devices  6.76 us (6%)
  other arithmetic  4.85 us (5%)
  waiting for transfers between devices  4.34 us (4%)
    all_to_all x1, blocking collectives, on_device(): lax.all_to_all(outgoing, 'node', split_axis=0, concat_axis=0, tiled=True)  50.1 us
    pallas_call x1, Pallas kernels, hist_and_best(): pl.pallas_call(histogram_kernel, grid_spec=pltpu.PrefetchScalarGridSpec(n...  13.4 us
    scatter x1, local copies, waits for them, and re-layouts, on_device(): outgoing = empty.T.at[position].set(payload.T, mode='drop')  12 us
    all_to_all x1, starting transfers between devices, on_device(): lax.all_to_all(best_spread, 'feat', split_axis=1, concat_axis=1, tiled=True)  6.76 us
    all_to_all x1, waiting for transfers between devices, on_device(): lax.all_to_all(best_spread, 'feat', split_axis=1, concat_axis=1, tiled=True)  4.34 us
    slice x3, local copies, waits for them, and re-layouts, on_device(): arrived[feat_count:]  2.13 us
    unnamed x6, local copies, waits for them, and re-layouts  2.13 us
  transfers between devices with their start and end apart: 1, of which 1 were waited for; matrix products, arithmetic and copies ran while one was open for 2% of the time, Pallas kernels for 0%

profile of v11, /device:TPU:1, one launch (start us, length us, event | category | flops | bytes accessed | tf_op | source)
XLA Modules:
  0.0 103.5 jit_solution(14570741165321649317)
XLA Ops:
  0.6 0.7 broadcast_compare_fusion
  1.4 1.0 select_reduce_fusion
  2.4 0.9 multiply_floor_fusion
  3.3 0.9 maximum_bitcast_fusion
  4.2 0.0 copy-start.1
  4.2 0.5 copy.20
  4.7 0.4 convolution_bitcast_fusion
  5.1 0.4 slice_reduce_fusion
  5.5 0.1 fusion.5
  5.6 0.4 multiply_reduce_fusion
  6.0 0.0 copy-done.1
  6.1 0.3 transpose.24
  6.4 12.0 %scatter_fusion = bf16[8192,32]{1,0:T(8,128)(2,1)S(1)} fusion(bf16[8192,32]{1,0:T(8,128)(2,1)S(1)} %transpose.24, s32[4096]{0:T(1024)S(1)} %compare_select_fusion, bf16[4096,32]{1,0:T(8,128)(2,1)S(1)} %copy.20), kind=kCustom, calls=%fused_computation | custom fusion | bytes 802816 | tf_op jit(solution)/shard_map/scatter | solution.py:107
  18.3 0.8 copy.21
  19.1 50.1 %all_to_all.10 = bf16[32,256,32]{1,2,0:T(8,128)(2,1)S(1)} all-to-all(bf16[32,256,32]{1,2,0:T(8,128)(2,1)S(1)} %copy.21), channel_id=1, replica_groups=mesh['node'=32,'feat'=16] {'node'}, dimensions={0} | all-to-all | bytes 1048576 | tf_op jit(solution)/shard_map/all_to_all | solution.py:109
  69.2 0.1 reshape.42
  69.3 0.4 fusion.6
  69.7 0.7 copy.23
  70.4 1.1 %slice.26 = bf16[16,2,4096]{2,0,1:T(8,128)(2,1)S(1)} reshape(bf16[16,2,128,32]{3,2,0,1:T(8,128)(2,1)S(1)} %copy.23) | data formatting | bytes 524288 | tf_op jit(solution)/shard_map/slice | solution.py:115
  71.5 0.7 copy.22
  72.2 1.1 %slice.23 = bf16[16,2,4096]{2,0,1:T(8,128)(2,1)S(1)} reshape(bf16[16,2,128,32]{3,2,0,1:T(8,128)(2,1)S(1)} %copy.22) | data formatting | bytes 524288 | tf_op jit(solution)/shard_map/slice | solution.py:112
  73.3 0.0 copy-start
  73.3 0.1 compare_reduce_fusion
  73.4 0.1 bitcast_reduce_fusion
  73.5 0.6 reshape.43.flags_ref
  74.1 0.8 concatenate.11.stats_ref
  74.9 0.0 copy-done
  75.0 13.4 %shard_map.68 = (f32[2,16,17,256]{3,2,1,0:T(8,128)}, f32[2,16,128]{2,1,0:T(8,128)}) custom-call(s32[32]{0:T(128)} %reshape.43.flags_ref, bf16[2,16,4096]{2,1,0:T(8,128)(2,1)} %bitcast.33, bf16[2,17,4096]{2,1,0:T(8,128)(2,1)} %concatenate.11.stats_ref), custom_call_target="tpu_custom_call" | custom-call | tf_op jit(solution)/shard_map/pallas_call | solution.py:55
  88.4 1.3 %copy.24 = f32[2,16,128]{2,0,1:T(2,128)} copy(f32[2,16,128]{2,1,0:T(8,128)} %get-tuple-element.5) | data formatting | bytes 32768 | tf_op jit(solution)/shard_map/pallas_call | solution.py:55
  89.7 6.8 %all-to-all-start.1 = ((f32[2,16,128]{2,0,1:T(2,128)}), f32[2,16,128]{2,0,1:T(2,128)S(1)}, u32[]{:S(2)}, u32[]{:S(2)}) async-start(f32[2,16,128]{2,0,1:T(2,128)} %copy.24), calls=%async_computation.1 | async-start | bytes 32768 | tf_op jit(solution)/shard_map/all_to_all | solution.py:117
  96.5 2.1 %copy.25 = f32[2,16,17,256]{3,1,2,0:T(8,128)} copy(f32[2,16,17,256]{3,2,1,0:T(8,128)} %get-tuple-element.12) | data formatting | bytes 1114112
  98.6 4.3 %all-to-all-done.1 = f32[2,16,128]{2,0,1:T(2,128)S(1)} async-done(((f32[2,16,128]{2,0,1:T(2,128)}), f32[2,16,128]{2,0,1:T(2,128)S(1)}, u32[]{:S(2)}, u32[]{:S(2)}) %all-to-all-start.1) | async-done | bytes 16416 | tf_op jit(solution)/shard_map/all_to_all | solution.py:117
  102.9 0.6 slice_reduce_fusion.1
  (8 shorter events, 0.1 us)
Async XLA Ops:
  4.2 1.8 %copy-start.1 = (s32[4096]{0:T(1024)S(1)}, s32[4096]{0:T(1024)}, u32[]{:S(2)}) copy-start(s32[4096]{0:T(1024)} %param.7) | copy-start | bytes 49156
  73.3 1.7 %copy-start = (bf16[16,2,4096]{2,0,1:T(8,128)(2,1)}, bf16[16,2,4096]{2,0,1:T(8,128)(2,1)S(1)}, u32[]{:S(2)}) copy-start(bf16[16,2,4096]{2,0,1:T(8,128)(2,1)S(1)} %slice.23) | copy-start | bytes 786436
  89.7 13.2 %all-to-all-start.1 = ((f32[2,16,128]{2,0,1:T(2,128)}), f32[2,16,128]{2,0,1:T(2,128)S(1)}, u32[]{:S(2)}, u32[]{:S(2)}) async-start(f32[2,16,128]{2,0,1:T(2,128)} %copy.24), calls=%async_computation.1 | async-start | bytes 32768 | tf_op jit(solution)/shard_map/all_to_all | solution.py:117

commit v12 on v10

--- a/solution.py
+++ b/solution.py
@@ -44,7 +44,7 @@
         right_part = jnp.sum(right[1:] * right[1:], axis=0, keepdims=True) / (right[0:1] + 1.0)
         total_part = jnp.sum(total[1:] * total[1:], axis=0, keepdims=True) / (total[0:1] + 1.0)
         best = jnp.maximum(best, left_part + right_part - total_part)
-    best_ref[0] = jnp.broadcast_to(jnp.max(best, axis=1, keepdims=True), best_ref.shape[1:])
+    best_ref[...] = jnp.broadcast_to(jnp.max(best, axis=1, keepdims=True), best_ref.shape)
 
 def hist_and_best(bins, stats, spread):
     nodes, feats, slots = bins.shape
@@ -60,9 +60,9 @@
             in_specs=[pl.BlockSpec((1, feats, slots), lambda n, fl: (n, 0, 0)),
                       pl.BlockSpec((1, st, slots), lambda n, fl: (n, 0, 0))],
             out_specs=[pl.BlockSpec((1, feats, st, B), lambda n, fl: (n, 0, 0, 0)),
-                       pl.BlockSpec((1, spread, 128), lambda n, fl: (n, 0, 0))]),
+                       pl.BlockSpec((spread, 1, 128), lambda n, fl: (0, 0, n))]),
         out_shape=[jax.ShapeDtypeStruct((nodes, feats, st, B), jnp.float32),
-                   jax.ShapeDtypeStruct((nodes, spread, 128), jnp.float32)])(flags, bins, stats)
+                   jax.ShapeDtypeStruct((spread, 1, nodes * 128), jnp.float32)])(flags, bins, stats)
     return hist, best
 
 
@@ -114,8 +114,8 @@
     ones = jnp.ones((node_local, 1, arrived.shape[2]), jnp.bfloat16)
     statistics = jnp.concatenate([ones, jnp.transpose(arrived[feat_count:], (1, 0, 2))], axis=1)
     histogram, best_spread = hist_and_best(bin_table, statistics, feat_devices)
-    gathered = lax.all_to_all(best_spread, "feat", split_axis=1, concat_axis=1, tiled=True)
-    best_gain = jnp.max(gathered[:, :, 0], axis=1)
+    gathered = lax.all_to_all(best_spread, "feat", split_axis=0, concat_axis=0, tiled=True)
+    best_gain = jnp.max(gathered.reshape(feat_devices, node_local, 128)[:, :, 0], axis=0)
     return (histogram, best_gain)
 
 

time: 106 us -> 104 us (0.981)
  Pallas kernels: 16.3 us -> 14.8 us
  local copies, waits for them, and re-layouts: 22.4 us -> 21.1 us
    pallas_call x1, Pallas kernels: 16.3 us -> 14.8 us  [hist_and_best(): pl.pallas_call(histogram_kernel, grid_spec=pltpu.PrefetchScalarGridSpec(n...]
    pallas_call x1 -> x0, local copies, waits for them, and re-layouts: 1.32 us -> none  [hist_and_best(): pl.pallas_call(histogram_kernel, grid_spec=pltpu.PrefetchScalarGridSpec(n...]
where the time goes in v12:
time: 104 us; the launch traced here: 103 us
  blocking collectives  50.1 us (48%)
  local copies, waits for them, and re-layouts  21.1 us (20%)
  Pallas kernels  14.8 us (14%)
  starting transfers between devices  6.75 us (6%)
  waiting for transfers between devices  4.43 us (4%)
  other arithmetic  4.41 us (4%)
    all_to_all x1, blocking collectives, on_device(): lax.all_to_all(outgoing, 'node', split_axis=0, concat_axis=0, tiled=True)  50.1 us
    pallas_call x1, Pallas kernels, hist_and_best(): pl.pallas_call(histogram_kernel, grid_spec=pltpu.PrefetchScalarGridSpec(n...  14.8 us
    scatter x1, local copies, waits for them, and re-layouts, on_device(): outgoing = empty.T.at[position].set(payload.T, mode='drop')  12 us
    all_to_all x1, starting transfers between devices, on_device(): lax.all_to_all(best_spread, 'feat', split_axis=0, concat_axis=0, tiled=True)  6.75 us
    all_to_all x1, waiting for transfers between devices, on_device(): lax.all_to_all(best_spread, 'feat', split_axis=0, concat_axis=0, tiled=True)  4.43 us
    unnamed x6, local copies, waits for them, and re-layouts  2.13 us
  transfers between devices with their start and end apart: 1, of which 1 were waited for; matrix products, arithmetic and copies ran while one was open for 2% of the time, Pallas kernels for 0%

profile of v12, /device:TPU:1, one launch (start us, length us, event | category | flops | bytes accessed | tf_op | source)
XLA Modules:
  0.0 102.9 jit_solution(6705702227368185241)
XLA Ops:
  0.6 0.7 broadcast_compare_fusion
  1.4 1.0 select_reduce_fusion
  2.4 1.0 maximum_bitcast_fusion
  3.3 0.0 copy-start.1
  3.4 0.5 copy.14
  3.8 0.4 convolution_bitcast_fusion
  4.2 0.4 slice_reduce_fusion
  4.6 0.1 fusion.6
  4.7 0.4 multiply_reduce_fusion
  5.2 0.0 copy-done.1
  5.2 0.3 transpose.24
  5.5 12.0 %scatter_fusion = bf16[8192,32]{1,0:T(8,128)(2,1)S(1)} fusion(bf16[8192,32]{1,0:T(8,128)(2,1)S(1)} %transpose.24, s32[4096]{0:T(1024)S(1)} %compare_select_fusion, bf16[4096,32]{1,0:T(8,128)(2,1)S(1)} %copy.14), kind=kCustom, calls=%fused_computation | custom fusion | bytes 802816 | tf_op jit(solution)/shard_map/scatter | solution.py:107
  17.5 0.8 copy.15
  18.3 50.1 %all_to_all.10 = bf16[32,256,32]{1,2,0:T(8,128)(2,1)S(1)} all-to-all(bf16[32,256,32]{1,2,0:T(8,128)(2,1)S(1)} %copy.15), channel_id=1, replica_groups=mesh['node'=32,'feat'=16] {'node'}, dimensions={0} | all-to-all | bytes 1048576 | tf_op jit(solution)/shard_map/all_to_all | solution.py:109
  68.3 0.1 reshape.48
  68.5 0.4 fusion.7
  68.9 0.7 copy.17
  69.6 1.1 %slice.23 = bf16[16,2,4096]{2,0,1:T(8,128)(2,1)S(1)} reshape(bf16[16,2,128,32]{3,2,0,1:T(8,128)(2,1)S(1)} %copy.17) | data formatting | bytes 524288 | tf_op jit(solution)/shard_map/slice | solution.py:115
  70.7 0.8 concatenate.11.stats_ref
  71.5 0.6 copy.16
  72.2 1.1 %floor.7 = bf16[16,2,4096]{2,0,1:T(8,128)(2,1)S(1)} reshape(bf16[16,2,128,32]{3,2,0,1:T(8,128)(2,1)S(1)} %copy.16) | data formatting | bytes 524288 | tf_op jit(solution)/shard_map/floor | solution.py:112
  73.3 0.0 copy-start
  73.3 0.1 compare_reduce_fusion
  73.4 0.1 bitcast_reduce_fusion
  73.5 0.6 reshape.50.flags_ref
  74.1 0.0 copy-done
  74.1 14.8 %shard_map.68 = (f32[2,16,17,256]{3,2,1,0:T(8,128)}, f32[16,1,256]{2,1,0:T(1,128)}) custom-call(s32[32]{0:T(128)} %reshape.50.flags_ref, bf16[2,16,4096]{2,1,0:T(8,128)(2,1)} %bitcast.34, bf16[2,17,4096]{2,1,0:T(8,128)(2,1)} %concatenate.11.stats_ref), custom_call_target="tpu_custom_call" | custom-call | tf_op jit(solution)/shard_map/pallas_call | solution.py:55
  89.0 6.8 %all-to-all-start.1 = ((f32[16,1,256]{2,1,0:T(1,128)}), f32[16,1,256]{2,1,0:T(1,128)S(1)}, u32[]{:S(2)}, u32[]{:S(2)}) async-start(f32[16,1,256]{2,1,0:T(1,128)} %get-tuple-element.5), calls=%async_computation.1 | async-start | bytes 32768 | tf_op jit(solution)/shard_map/all_to_all | solution.py:117
  95.7 2.1 %copy.18 = f32[2,16,17,256]{3,1,2,0:T(8,128)} copy(f32[2,16,17,256]{3,2,1,0:T(8,128)} %get-tuple-element.10) | data formatting | bytes 1114112
  97.8 4.4 %all-to-all-done.1 = f32[16,1,256]{2,1,0:T(1,128)S(1)} async-done(((f32[16,1,256]{2,1,0:T(1,128)}), f32[16,1,256]{2,1,0:T(1,128)S(1)}, u32[]{:S(2)}, u32[]{:S(2)}) %all-to-all-start.1) | async-done | bytes 16416 | tf_op jit(solution)/shard_map/all_to_all | solution.py:117
  102.3 0.6 slice_reduce_fusion.1
  (8 shorter events, 0.1 us)
Async XLA Ops:
  3.3 1.8 %copy-start.1 = (s32[4096]{0:T(1024)S(1)}, s32[4096]{0:T(1024)}, u32[]{:S(2)}) copy-start(s32[4096]{0:T(1024)} %param.7) | copy-start | bytes 49156
  73.3 0.9 copy-start
  89.0 13.3 %all-to-all-start.1 = ((f32[16,1,256]{2,1,0:T(1,128)}), f32[16,1,256]{2,1,0:T(1,128)S(1)}, u32[]{:S(2)}, u32[]{:S(2)}) async-start(f32[16,1,256]{2,1,0:T(1,128)} %get-tuple-element.5), calls=%async_computation.1 | async-start | bytes 32768 | tf_op jit(solution)/shard_map/all_to_all | solution.py:117

commit v13 on v12

--- a/solution.py
+++ b/solution.py
@@ -46,12 +46,10 @@
         best = jnp.maximum(best, left_part + right_part - total_part)
     best_ref[...] = jnp.broadcast_to(jnp.max(best, axis=1, keepdims=True), best_ref.shape)
 
-def hist_and_best(bins, stats, spread):
+def hist_and_best(bins, stats, spread, flags):
     nodes, feats, slots = bins.shape
     st = stats.shape[1]
     chunks = slots // CH
-    filled = jnp.any(bins[:, 0].reshape(nodes, chunks, CH) < B, axis=2)
-    flags = filled.astype(jnp.int32).reshape(nodes * chunks)
     hist, best = pl.pallas_call(
         histogram_kernel,
         grid_spec=pltpu.PrefetchScalarGridSpec(
@@ -108,12 +106,14 @@
     outgoing = outgoing.reshape(node_devices, node_local * capacity, payload_width)
     arrived = lax.all_to_all(outgoing, "node", split_axis=0, concat_axis=0, tiled=True)
     arrived = arrived.reshape(node_devices, node_local, capacity, payload_width)
+    firsts = arrived[:, :, :, 0].reshape(node_devices, node_local * capacity * node_devices // CH, CH // node_devices)
+    flags = jnp.any(firsts < B, axis=(0, 2)).astype(jnp.int32)
     arrived = jnp.transpose(arrived, (3, 1, 2, 0)).reshape(payload_width, node_local, capacity * node_devices)
     bin_table = jnp.floor(arrived[:feat_count] * B)
     bin_table = jnp.transpose(bin_table, (1, 0, 2))
     ones = jnp.ones((node_local, 1, arrived.shape[2]), jnp.bfloat16)
     statistics = jnp.concatenate([ones, jnp.transpose(arrived[feat_count:], (1, 0, 2))], axis=1)
-    histogram, best_spread = hist_and_best(bin_table, statistics, feat_devices)
+    histogram, best_spread = hist_and_best(bin_table, statistics, feat_devices, flags)
     gathered = lax.all_to_all(best_spread, "feat", split_axis=0, concat_axis=0, tiled=True)
     best_gain = jnp.max(gathered.reshape(feat_devices, node_local, 128)[:, :, 0], axis=0)
     return (histogram, best_gain)

time: 104 us -> 118 us (1.13)
  Pallas kernels: 14.8 us -> 29.3 us
    pallas_call x1, Pallas kernels: 14.8 us -> 29.3 us  [hist_and_best(): pl.pallas_call(histogram_kernel, grid_spec=pltpu.PrefetchScalarGridSpec(n...]
where the time goes in v13:
time: 118 us
  blocking collectives  50.1 us (42%)
  Pallas kernels  29.3 us (25%)
  local copies, waits for them, and re-layouts  21.3 us (18%)
  starting transfers between devices  6.75 us (6%)
  other arithmetic  4.86 us (4%)
  waiting for transfers between devices  4.34 us (4%)
    all_to_all x1, blocking collectives, on_device(): lax.all_to_all(outgoing, 'node', split_axis=0, concat_axis=0, tiled=True)  50.1 us
    pallas_call x1, Pallas kernels, hist_and_best(): pl.pallas_call(histogram_kernel, grid_spec=pltpu.PrefetchScalarGridSpec(n...  29.3 us
    scatter x1, local copies, waits for them, and re-layouts, on_device(): outgoing = empty.T.at[position].set(payload.T, mode='drop')  12 us
    all_to_all x1, starting transfers between devices, on_device(): lax.all_to_all(best_spread, 'feat', split_axis=0, concat_axis=0, tiled=True)  6.75 us
    all_to_all x1, waiting for transfers between devices, on_device(): lax.all_to_all(best_spread, 'feat', split_axis=0, concat_axis=0, tiled=True)  4.34 us
    floor x2, local copies, waits for them, and re-layouts, on_device(): bin_table = jnp.floor(arrived[:feat_count] * B)  2.48 us
  transfers between devices with their start and end apart: 1, of which 1 were waited for; matrix products, arithmetic and copies ran while one was open for 2% of the time, Pallas kernels for 0%

profile of v13, /device:TPU:1, one launch (start us, length us, event | category | flops | bytes accessed | tf_op | source)
XLA Modules:
  0.0 117.9 jit_solution(5699183737985981990)
XLA Ops:
  0.6 0.7 broadcast_compare_fusion
  1.4 1.0 select_reduce_fusion
  2.4 1.0 maximum_bitcast_fusion
  3.3 0.0 copy-start
  3.4 0.5 copy.14
  3.8 0.4 convolution_bitcast_fusion
  4.2 0.4 slice_reduce_fusion
  4.6 0.1 fusion.6
  4.7 0.4 multiply_reduce_fusion
  5.2 0.0 copy-done
  5.2 0.3 transpose.24
  5.5 12.0 %scatter_fusion = bf16[8192,32]{1,0:T(8,128)(2,1)S(1)} fusion(bf16[8192,32]{1,0:T(8,128)(2,1)S(1)} %transpose.24, s32[4096]{0:T(1024)S(1)} %compare_select_fusion, bf16[4096,32]{1,0:T(8,128)(2,1)S(1)} %copy.14), kind=kCustom, calls=%fused_computation | custom fusion | bytes 802816 | tf_op jit(solution)/shard_map/scatter | solution.py:105
  17.5 0.8 copy.15
  18.3 50.1 %all_to_all.10 = bf16[32,256,32]{1,2,0:T(8,128)(2,1)S(1)} all-to-all(bf16[32,256,32]{1,2,0:T(8,128)(2,1)S(1)} %copy.15), channel_id=1, replica_groups=mesh['node'=32,'feat'=16] {'node'}, dimensions={0} | all-to-all | bytes 1048576 | tf_op jit(solution)/shard_map/all_to_all | solution.py:107
  68.3 0.1 reshape.43
  68.5 0.1 reduce_or.14
  68.6 0.1 reduce_or.18
  68.7 0.5 convert_element_type.24.flags_ref
  69.3 0.4 fusion.7
  69.7 0.7 copy.17
  70.4 1.1 slice.23
  71.5 0.8 concatenate.11.stats_ref
  72.3 0.6 copy.16
  72.9 1.8 %floor.7 = bf16[16,2,4096]{2,0,1:T(8,128)(2,1)} reshape(bf16[16,2,128,32]{3,2,0,1:T(8,128)(2,1)S(1)} %copy.16) | data formatting | bytes 524288 | tf_op jit(solution)/shard_map/floor | solution.py:112
  74.8 29.3 %shard_map.68 = (f32[2,16,17,256]{3,2,1,0:T(8,128)}, f32[16,1,256]{2,1,0:T(1,128)}) custom-call(s32[32]{0:T(128)} %convert_element_type.24.flags_ref, bf16[2,16,4096]{2,1,0:T(8,128)(2,1)} %bitcast.30, bf16[2,17,4096]{2,1,0:T(8,128)(2,1)} %concatenate.11.stats_ref), custom_call_target="tpu_custom_call" | custom-call | tf_op jit(solution)/shard_map/pallas_call | solution.py:53
  104.1 6.8 %all-to-all-start.1 = ((f32[16,1,256]{2,1,0:T(1,128)}), f32[16,1,256]{2,1,0:T(1,128)S(1)}, u32[]{:S(2)}, u32[]{:S(2)}) async-start(f32[16,1,256]{2,1,0:T(1,128)} %get-tuple-element.5), calls=%async_computation.1 | async-start | bytes 32768 | tf_op jit(solution)/shard_map/all_to_all | solution.py:117
  110.8 2.1 %copy.18 = f32[2,16,17,256]{3,1,2,0:T(8,128)} copy(f32[2,16,17,256]{3,2,1,0:T(8,128)} %get-tuple-element.10) | data formatting | bytes 1114112
  112.9 4.3 %all-to-all-done.1 = f32[16,1,256]{2,1,0:T(1,128)S(1)} async-done(((f32[16,1,256]{2,1,0:T(1,128)}), f32[16,1,256]{2,1,0:T(1,128)S(1)}, u32[]{:S(2)}, u32[]{:S(2)}) %all-to-all-start.1) | async-done | bytes 16416 | tf_op jit(solution)/shard_map/all_to_all | solution.py:117
  117.3 0.6 slice_reduce_fusion.1
  (8 shorter events, 0.1 us)
Async XLA Ops:
  3.3 1.8 %copy-start = (s32[4096]{0:T(1024)S(1)}, s32[4096]{0:T(1024)}, u32[]{:S(2)}) copy-start(s32[4096]{0:T(1024)} %param.7) | copy-start | bytes 49156
  104.1 13.2 %all-to-all-start.1 = ((f32[16,1,256]{2,1,0:T(1,128)}), f32[16,1,256]{2,1,0:T(1,128)S(1)}, u32[]{:S(2)}, u32[]{:S(2)}) async-start(f32[16,1,256]{2,1,0:T(1,128)} %get-tuple-element.5), calls=%async_computation.1 | async-start | bytes 32768 | tf_op jit(solution)/shard_map/all_to_all | solution.py:117

commit v14 on v12

--- a/solution.py
+++ b/solution.py
@@ -99,7 +99,8 @@
     rank = running_rank(owned)
     slots = node_total * capacity
     position = jnp.where(kept, target * capacity + rank, slots)
-    payload = jnp.concatenate([covariates, pseudo], axis=0)
+    weight_row = jnp.ones((1, row_count), jnp.bfloat16)
+    payload = jnp.concatenate([covariates, weight_row, pseudo], axis=0)
     payload_width = payload.shape[0]
     empty = jnp.concatenate(
         [jnp.ones((feat_count, slots), jnp.bfloat16), jnp.zeros((payload_width - feat_count, slots), jnp.bfloat16)]
@@ -111,8 +112,7 @@
     arrived = jnp.transpose(arrived, (3, 1, 2, 0)).reshape(payload_width, node_local, capacity * node_devices)
     bin_table = jnp.floor(arrived[:feat_count] * B)
     bin_table = jnp.transpose(bin_table, (1, 0, 2))
-    ones = jnp.ones((node_local, 1, arrived.shape[2]), jnp.bfloat16)
-    statistics = jnp.concatenate([ones, jnp.transpose(arrived[feat_count:], (1, 0, 2))], axis=1)
+    statistics = jnp.transpose(arrived[feat_count:], (1, 0, 2))
     histogram, best_spread = hist_and_best(bin_table, statistics, feat_devices)
     gathered = lax.all_to_all(best_spread, "feat", split_axis=0, concat_axis=0, tiled=True)
     best_gain = jnp.max(gathered.reshape(feat_devices, node_local, 128)[:, :, 0], axis=0)

time: 104 us -> 109 us (1.048)
  blocking collectives: 50.1 us -> 55.6 us
  local copies, waits for them, and re-layouts: 21.1 us -> 23 us
  Pallas kernels: 14.8 us -> 13.4 us
    all_to_all x1, blocking collectives: 50.1 us -> 55.6 us  [on_device(): lax.all_to_all(outgoing, 'node', split_axis=0, concat_axis=0, tiled=True)]
    slice x2 -> x3, local copies, waits for them, and re-layouts: 1.76 us -> 3.46 us  [on_device(): statistics = jnp.transpose(arrived[feat_count:], (1, 0, 2))]
    pallas_call x1, Pallas kernels: 14.8 us -> 13.4 us  [hist_and_best(): pl.pallas_call(histogram_kernel, grid_spec=pltpu.PrefetchScalarGridSpec(n...]
where the time goes in v14:
time: 109 us
  blocking collectives  55.6 us (51%)
  local copies, waits for them, and re-layouts  23 us (21%)
  Pallas kernels  13.4 us (12%)
  starting transfers between devices  6.74 us (6%)
  other arithmetic  4.39 us (4%)
  waiting for transfers between devices  4.34 us (4%)
    all_to_all x1, blocking collectives, on_device(): lax.all_to_all(outgoing, 'node', split_axis=0, concat_axis=0, tiled=True)  55.6 us
    pallas_call x1, Pallas kernels, hist_and_best(): pl.pallas_call(histogram_kernel, grid_spec=pltpu.PrefetchScalarGridSpec(n...  13.4 us
    scatter x1, local copies, waits for them, and re-layouts, on_device(): outgoing = empty.T.at[position].set(payload.T, mode='drop')  12 us
    all_to_all x1, starting transfers between devices, on_device(): lax.all_to_all(best_spread, 'feat', split_axis=0, concat_axis=0, tiled=True)  6.74 us
    all_to_all x1, waiting for transfers between devices, on_device(): lax.all_to_all(best_spread, 'feat', split_axis=0, concat_axis=0, tiled=True)  4.34 us
    slice x3, local copies, waits for them, and re-layouts, on_device(): statistics = jnp.transpose(arrived[feat_count:], (1, 0, 2))  3.46 us
  transfers between devices with their start and end apart: 1, of which 1 were waited for; matrix products, arithmetic and copies ran while one was open for 2% of the time, Pallas kernels for 0%

profile of v14, /device:TPU:1, one launch (start us, length us, event | category | flops | bytes accessed | tf_op | source)
XLA Modules:
  0.0 108.8 jit_solution(1604316254063145806)
XLA Ops:
  0.6 0.7 broadcast_compare_fusion
  1.4 1.0 select_reduce_fusion
  2.4 0.1 pad.2.clone
  2.4 1.1 maximum_bitcast_fusion
  3.5 0.0 copy-start.1
  3.5 0.5 copy.22
  4.0 0.4 convolution_bitcast_fusion
  4.4 0.4 slice_reduce_fusion
  4.8 0.1 fusion.6
  4.9 0.4 multiply_reduce_fusion
  5.3 0.0 copy-done.1
  5.4 0.3 transpose.24
  5.7 12.0 %scatter_fusion = bf16[8192,33]{1,0:T(8,128)(2,1)S(1)} fusion(bf16[8192,33]{1,0:T(8,128)(2,1)S(1)} %transpose.24, s32[4096]{0:T(1024)S(1)} %compare_select_fusion, bf16[4096,33]{1,0:T(8,128)(2,1)S(1)} %copy.22), kind=kCustom, calls=%fused_computation | custom fusion | bytes 827392 | tf_op jit(solution)/shard_map/scatter | solution.py:108
  17.6 1.0 copy.23
  18.6 55.6 %all_to_all.10 = bf16[32,256,33]{1,2,0:T(8,128)(2,1)S(1)} all-to-all(bf16[32,256,33]{1,2,0:T(8,128)(2,1)S(1)} %copy.23), channel_id=1, replica_groups=mesh['node'=32,'feat'=16] {'node'}, dimensions={0} | all-to-all | bytes 1081344 | tf_op jit(solution)/shard_map/all_to_all | solution.py:110
  74.3 0.3 reshape.61
  74.6 0.6 copy.36
  75.1 0.3 fusion.3
  75.5 0.2 slice.28
  75.7 0.6 copy.25
  76.3 1.1 %floor.7 = bf16[16,2,4096]{2,0,1:T(8,128)(2,1)S(1)} reshape(bf16[16,2,128,32]{3,2,0,1:T(8,128)(2,1)S(1)} %copy.25) | data formatting | bytes 524288 | tf_op jit(solution)/shard_map/floor | solution.py:113
  77.5 0.0 copy-start
  77.5 0.1 compare_reduce_fusion
  77.6 0.1 bitcast_reduce_fusion
  77.7 0.6 reshape.50.flags_ref
  78.3 1.2 %copy.30 = bf16[17,2,128,32]{3,2,0,1:T(8,128)(2,1)S(1)} copy(bf16[17,2,128,32]{2,1,3,0:T(2,128)(2,1)S(1)} %slice.28) | data formatting | bytes 557056 | tf_op jit(solution)/shard_map/slice | solution.py:115
  79.5 2.0 %reshape.62 = bf16[17,2,4096]{2,0,1:T(8,128)(2,1)} reshape(bf16[17,2,128,32]{3,2,0,1:T(8,128)(2,1)S(1)} %copy.30) | data formatting | bytes 557056 | tf_op jit(solution)/shard_map/slice | solution.py:115
  81.5 0.0 copy-done
  81.5 13.4 %shard_map.68 = (f32[2,16,17,256]{3,2,1,0:T(8,128)}, f32[16,1,256]{2,1,0:T(1,128)}) custom-call(s32[32]{0:T(128)} %reshape.50.flags_ref, bf16[2,16,4096]{2,1,0:T(8,128)(2,1)} %bitcast.39, bf16[2,17,4096]{2,1,0:T(8,128)(2,1)} %bitcast.37), custom_call_target="tpu_custom_call" | custom-call | tf_op jit(solution)/shard_map/pallas_call | solution.py:55
  95.0 6.7 %all-to-all-start.1 = ((f32[16,1,256]{2,1,0:T(1,128)}), f32[16,1,256]{2,1,0:T(1,128)S(1)}, u32[]{:S(2)}, u32[]{:S(2)}) async-start(f32[16,1,256]{2,1,0:T(1,128)} %get-tuple-element.5), calls=%async_computation.1 | async-start | bytes 32768 | tf_op jit(solution)/shard_map/all_to_all | solution.py:117
  101.7 2.1 %copy.28 = f32[2,16,17,256]{3,1,2,0:T(8,128)} copy(f32[2,16,17,256]{3,2,1,0:T(8,128)} %get-tuple-element.12) | data formatting | bytes 1114112
  103.8 4.3 %all-to-all-done.1 = f32[16,1,256]{2,1,0:T(1,128)S(1)} async-done(((f32[16,1,256]{2,1,0:T(1,128)}), f32[16,1,256]{2,1,0:T(1,128)S(1)}, u32[]{:S(2)}, u32[]{:S(2)}) %all-to-all-start.1) | async-done | bytes 16416 | tf_op jit(solution)/shard_map/all_to_all | solution.py:117
  108.2 0.6 slice_reduce_fusion.1
  (8 shorter events, 0.1 us)
Async XLA Ops:
  3.5 1.8 %copy-start.1 = (s32[4096]{0:T(1024)S(1)}, s32[4096]{0:T(1024)}, u32[]{:S(2)}) copy-start(s32[4096]{0:T(1024)} %param.7) | copy-start | bytes 49156
  77.5 4.1 %copy-start = (bf16[16,2,4096]{2,0,1:T(8,128)(2,1)}, bf16[16,2,4096]{2,0,1:T(8,128)(2,1)S(1)}, u32[]{:S(2)}) copy-start(bf16[16,2,4096]{2,0,1:T(8,128)(2,1)S(1)} %floor.7) | copy-start | bytes 786436
  95.0 13.2 %all-to-all-start.1 = ((f32[16,1,256]{2,1,0:T(1,128)}), f32[16,1,256]{2,1,0:T(1,128)S(1)}, u32[]{:S(2)}, u32[]{:S(2)}) async-start(f32[16,1,256]{2,1,0:T(1,128)} %get-tuple-element.5), calls=%async_computation.1 | async-start | bytes 32768 | tf_op jit(solution)/shard_map/all_to_all | solution.py:117

commit v15 on v12

--- a/solution.py
+++ b/solution.py
@@ -99,17 +99,17 @@
     rank = running_rank(owned)
     slots = node_total * capacity
     position = jnp.where(kept, target * capacity + rank, slots)
-    payload = jnp.concatenate([covariates, pseudo], axis=0)
+    payload = jnp.concatenate([jnp.floor(covariates * B), pseudo], axis=0)
     payload_width = payload.shape[0]
     empty = jnp.concatenate(
-        [jnp.ones((feat_count, slots), jnp.bfloat16), jnp.zeros((payload_width - feat_count, slots), jnp.bfloat16)]
+        [jnp.full((feat_count, slots), B, jnp.bfloat16), jnp.zeros((payload_width - feat_count, slots), jnp.bfloat16)]
     )
     outgoing = empty.T.at[position].set(payload.T, mode="drop")
     outgoing = outgoing.reshape(node_devices, node_local * capacity, payload_width)
     arrived = lax.all_to_all(outgoing, "node", split_axis=0, concat_axis=0, tiled=True)
     arrived = arrived.reshape(node_devices, node_local, capacity, payload_width)
     arrived = jnp.transpose(arrived, (3, 1, 2, 0)).reshape(payload_width, node_local, capacity * node_devices)
-    bin_table = jnp.floor(arrived[:feat_count] * B)
+    bin_table = arrived[:feat_count]
     bin_table = jnp.transpose(bin_table, (1, 0, 2))
     ones = jnp.ones((node_local, 1, arrived.shape[2]), jnp.bfloat16)
     statistics = jnp.concatenate([ones, jnp.transpose(arrived[feat_count:], (1, 0, 2))], axis=1)

time: 104 us -> 106 us (1.019)
  Pallas kernels: 14.8 us -> 17 us
    pallas_call x1, Pallas kernels: 14.8 us -> 17 us  [hist_and_best(): pl.pallas_call(histogram_kernel, grid_spec=pltpu.PrefetchScalarGridSpec(n...]
    slice x0 -> x2, local copies, waits for them, and re-layouts: none -> 1.76 us  [on_device(): bin_table = arrived[:feat_count]]
    floor x2 -> x0, local copies, waits for them, and re-layouts: 1.75 us -> none  [on_device(): bin_table = jnp.floor(arrived[:feat_count] * B)]
    slice x2 -> x3, local copies, waits for them, and re-layouts: 1.76 us -> 2.13 us  [on_device(): arrived[feat_count:]]
where the time goes in v15:
time: 106 us
  blocking collectives  50.1 us (47%)
  local copies, waits for them, and re-layouts  21.5 us (20%)
  Pallas kernels  17 us (16%)
  starting transfers between devices  6.75 us (6%)
  other arithmetic  4.85 us (5%)
  waiting for transfers between devices  4.34 us (4%)
    all_to_all x1, blocking collectives, on_device(): lax.all_to_all(outgoing, 'node', split_axis=0, concat_axis=0, tiled=True)  50.1 us
    pallas_call x1, Pallas kernels, hist_and_best(): pl.pallas_call(histogram_kernel, grid_spec=pltpu.PrefetchScalarGridSpec(n...  17 us
    scatter x1, local copies, waits for them, and re-layouts, on_device(): outgoing = empty.T.at[position].set(payload.T, mode='drop')  12 us
    all_to_all x1, starting transfers between devices, on_device(): lax.all_to_all(best_spread, 'feat', split_axis=0, concat_axis=0, tiled=True)  6.75 us
    all_to_all x1, waiting for transfers between devices, on_device(): lax.all_to_all(best_spread, 'feat', split_axis=0, concat_axis=0, tiled=True)  4.34 us
    slice x3, local copies, waits for them, and re-layouts, on_device(): arrived[feat_count:]  2.13 us
    unnamed x6, local copies, waits for them, and re-layouts  2.13 us
  transfers between devices with their start and end apart: 1, of which 1 were waited for; matrix products, arithmetic and copies ran while one was open for 2% of the time, Pallas kernels for 0%

profile of v15, /device:TPU:1, one launch (start us, length us, event | category | flops | bytes accessed | tf_op | source)
XLA Modules:
  0.0 105.8 jit_solution(10561072781364039558)
XLA Ops:
  0.6 0.7 broadcast_compare_fusion
  1.4 1.0 select_reduce_fusion
  2.4 0.9 multiply_floor_fusion
  3.3 0.9 maximum_bitcast_fusion
  4.2 0.0 copy-start.1
  4.2 0.5 copy.14
  4.7 0.4 convolution_bitcast_fusion
  5.1 0.4 slice_reduce_fusion
  5.5 0.1 fusion.5
  5.6 0.4 multiply_reduce_fusion
  6.0 0.0 copy-done.1
  6.1 0.3 transpose.24
  6.4 12.0 %scatter_fusion = bf16[8192,32]{1,0:T(8,128)(2,1)S(1)} fusion(bf16[8192,32]{1,0:T(8,128)(2,1)S(1)} %transpose.24, s32[4096]{0:T(1024)S(1)} %compare_select_fusion, bf16[4096,32]{1,0:T(8,128)(2,1)S(1)} %copy.14), kind=kCustom, calls=%fused_computation | custom fusion | bytes 802816 | tf_op jit(solution)/shard_map/scatter | solution.py:107
  18.3 0.8 copy.15
  19.1 50.1 %all_to_all.10 = bf16[32,256,32]{1,2,0:T(8,128)(2,1)S(1)} all-to-all(bf16[32,256,32]{1,2,0:T(8,128)(2,1)S(1)} %copy.15), channel_id=1, replica_groups=mesh['node'=32,'feat'=16] {'node'}, dimensions={0} | all-to-all | bytes 1048576 | tf_op jit(solution)/shard_map/all_to_all | solution.py:109
  69.2 0.1 reshape.45
  69.3 0.4 fusion.6
  69.7 0.7 copy.17
  70.4 1.1 %slice.26 = bf16[16,2,4096]{2,0,1:T(8,128)(2,1)S(1)} reshape(bf16[16,2,128,32]{3,2,0,1:T(8,128)(2,1)S(1)} %copy.17) | data formatting | bytes 524288 | tf_op jit(solution)/shard_map/slice | solution.py:115
  71.5 0.7 copy.16
  72.2 1.1 %slice.23 = bf16[16,2,4096]{2,0,1:T(8,128)(2,1)S(1)} reshape(bf16[16,2,128,32]{3,2,0,1:T(8,128)(2,1)S(1)} %copy.16) | data formatting | bytes 524288 | tf_op jit(solution)/shard_map/slice | solution.py:112
  73.3 0.0 copy-start
  73.3 0.1 compare_reduce_fusion
  73.4 0.1 bitcast_reduce_fusion
  73.5 0.6 reshape.47.flags_ref
  74.1 0.8 concatenate.11.stats_ref
  75.0 0.0 copy-done
  75.0 17.0 %shard_map.68 = (f32[2,16,17,256]{3,2,1,0:T(8,128)}, f32[16,1,256]{2,1,0:T(1,128)}) custom-call(s32[32]{0:T(128)} %reshape.47.flags_ref, bf16[2,16,4096]{2,1,0:T(8,128)(2,1)} %bitcast.34, bf16[2,17,4096]{2,1,0:T(8,128)(2,1)} %concatenate.11.stats_ref), custom_call_target="tpu_custom_call" | custom-call | tf_op jit(solution)/shard_map/pallas_call | solution.py:55
  92.0 6.8 %all-to-all-start.1 = ((f32[16,1,256]{2,1,0:T(1,128)}), f32[16,1,256]{2,1,0:T(1,128)S(1)}, u32[]{:S(2)}, u32[]{:S(2)}) async-start(f32[16,1,256]{2,1,0:T(1,128)} %get-tuple-element.5), calls=%async_computation.1 | async-start | bytes 32768 | tf_op jit(solution)/shard_map/all_to_all | solution.py:117
  98.7 2.1 %copy.18 = f32[2,16,17,256]{3,1,2,0:T(8,128)} copy(f32[2,16,17,256]{3,2,1,0:T(8,128)} %get-tuple-element.10) | data formatting | bytes 1114112
  100.8 4.3 %all-to-all-done.1 = f32[16,1,256]{2,1,0:T(1,128)S(1)} async-done(((f32[16,1,256]{2,1,0:T(1,128)}), f32[16,1,256]{2,1,0:T(1,128)S(1)}, u32[]{:S(2)}, u32[]{:S(2)}) %all-to-all-start.1) | async-done | bytes 16416 | tf_op jit(solution)/shard_map/all_to_all | solution.py:117
  105.2 0.6 slice_reduce_fusion.1
  (8 shorter events, 0.1 us)
Async XLA Ops:
  4.2 1.8 %copy-start.1 = (s32[4096]{0:T(1024)S(1)}, s32[4096]{0:T(1024)}, u32[]{:S(2)}) copy-start(s32[4096]{0:T(1024)} %param.7) | copy-start | bytes 49156
  73.3 1.7 %copy-start = (bf16[16,2,4096]{2,0,1:T(8,128)(2,1)}, bf16[16,2,4096]{2,0,1:T(8,128)(2,1)S(1)}, u32[]{:S(2)}) copy-start(bf16[16,2,4096]{2,0,1:T(8,128)(2,1)S(1)} %slice.23) | copy-start | bytes 786436
  92.0 13.2 %all-to-all-start.1 = ((f32[16,1,256]{2,1,0:T(1,128)}), f32[16,1,256]{2,1,0:T(1,128)S(1)}, u32[]{:S(2)}, u32[]{:S(2)}) async-start(f32[16,1,256]{2,1,0:T(1,128)} %get-tuple-element.5), calls=%async_computation.1 | async-start | bytes 32768 | tf_op jit(solution)/shard_map/all_to_all | solution.py:117
